TPU v7x, 256 devices: a whole 4x4x8 slice. The times are simulated.
256 devices in a mesh: seq: 32 (over x, z), mp: 8 (over y, core).
Axes of the slice: x: 4, y: 4, z: 8, core: 2. Of those that a mesh axis runs over, the one named last changes fastest.
Arguments:
- frames: bfloat16 [36864, 1024], P('seq', 'mp'), may hold values from -6 to 6
- keep_flags: int32 [36864], P('seq'), may hold values from 0 to 1, as said below
- pack_rows: int32 [12288], P('seq'), may hold values from 0 to 12287, as said below
- ln_gains: float32 [2, 1024], replicated, may hold values from 0.25 to 1.75
- w_qkv: bfloat16 [1024, 3, 1024], P(None, None, 'mp'), may hold values from -0.1875 to 0.1875, as said below
- w_attn_out: bfloat16 [1024, 1024], P('mp'), may hold values from -0.5 to 0.5
- w_up: bfloat16 [1024, 4096], P(None, 'mp'), may hold values from -0.1875 to 0.1875
- w_down: bfloat16 [4096, 1024], P('mp'), may hold values from -0.09375 to 0.09375
- mask_emb: bfloat16 [1024], replicated, may hold values from -5 to 5
- w_dec_in: bfloat16 [1024, 768], P(None, 'mp'), may hold values from -0.1875 to 0.1875
- w_conv: bfloat16 [4, 7, 768, 48], P(None, None, 'mp'), may hold values from -0.3125 to 0.3125
- w_dec_out: bfloat16 [768, 1024], P('mp'), may hold values from -0.21875 to 0.21875
- targets: bfloat16 [1024, 36864], P('mp', 'seq'), may hold values from -6 to 6
Outputs:
- student_rows: bfloat16 [12288, 1024], P('seq', 'mp')
- pred_error: bfloat16 [1024, 36864], P('mp', 'seq')
Inputs may be any that keep to these rules, and one draw needn't show every extreme that they name: `keep_flags`: in each aligned group of four blocks of 1152 frames exactly 1536 frames are kept, and no block keeps more than 768; in some group the first block keeps exactly 768. In all 12288 frames are kept. `pack_rows`: each aligned block of 384 entries is a permutation of the same block of packed rows. `w_qkv`: entries are of the size of a projection with 1024 inputs.
All inputs are finite; a program needn't handle non-finite values.
Results may differ from a plain program's by a relative error of at most 0.019.
Values may be sent and summed in bfloat16 or wider, within the bound.
No kernel may reach another device: no remote copies, remote signals or barrier semaphores. Data moves between devices by JAX's collectives and lax.ppermute only.
A program may use at most 64 MiB of HBM per device.

v0:
```python
import math

import jax
import jax.numpy as jnp
from jax import lax
from jax.sharding import PartitionSpec as P

HEAD_DIM = 64
C = 768
CG = 48
KW = 7
BLOCKS = 4


NORM_EPSILON = 1e-05


def with_halo(block, sides, width):
    for axis, dim in sides:
        count = lax.axis_size(axis)
        forward = [(i, i + 1) for i in range(count - 1)]
        backward = [(target, source) for source, target in forward]
        low = lax.ppermute(
            lax.slice_in_dim(block, block.shape[dim] - width, None, axis=dim), axis, forward
        )
        high = lax.ppermute(lax.slice_in_dim(block, 0, width, axis=dim), axis, backward)
        block = jnp.concatenate([low, block, high], axis=dim)
    return block


def layer_norm(values, gain):
    values = values.astype(jnp.float32)
    centre = jnp.mean(values, axis=-1, keepdims=True)
    spread = jnp.mean(jnp.square(values - centre), axis=-1, keepdims=True)
    return (values - centre) * lax.rsqrt(spread + NORM_EPSILON) * gain


def rounded(values):
    return lax.optimization_barrier(values.astype(jnp.bfloat16)).astype(jnp.float32)


def local(
    frames,
    keep_flags,
    pack_rows,
    ln_gains,
    w_qkv,
    w_attn_out,
    w_up,
    w_down,
    mask_emb,
    w_dec_in,
    w_conv,
    w_dec_out,
    targets,
):
    frame_count = keep_flags.shape[0]
    slot_rows = pack_rows.shape[0]
    feature_width = frames.shape[1]
    seq_devices = lax.axis_size("seq")
    seq_index = lax.axis_index("seq")
    capacity = (2 * slot_rows + seq_devices - 1) // seq_devices
    kept_count = jnp.sum(keep_flags)
    counts_all = lax.all_gather(kept_count[None], "seq", axis=0, tiled=True)
    starts_all = jnp.cumsum(counts_all) - counts_all
    kept_before = starts_all[seq_index]
    local_rank = jnp.cumsum(keep_flags) - keep_flags
    frame_index = jnp.arange(frame_count, dtype=jnp.int32)
    kept_where = (
        jnp.zeros((frame_count,), jnp.int32)
        .at[jnp.where(keep_flags == 1, local_rank, frame_count)]
        .set(frame_index, mode="drop")
    )
    global_rank = kept_before + local_rank
    slot_steps = jnp.arange(capacity, dtype=jnp.int32)[None, :] * seq_devices
    owners = jnp.arange(seq_devices, dtype=jnp.int32)
    first_sent = kept_before + (owners - kept_before) % seq_devices
    offset = first_sent[:, None] + slot_steps - kept_before
    inside = offset < kept_count
    source = kept_where[jnp.clip(offset, 0, frame_count - 1)]
    outgoing = jnp.where(inside[..., None], frames[source], jnp.zeros((), jnp.bfloat16))
    incoming = lax.all_to_all(outgoing, "seq", split_axis=0, concat_axis=0, tiled=True)
    first_got = starts_all + (seq_index - starts_all) % seq_devices
    ranks_got = first_got[:, None] + slot_steps
    valid = ranks_got < (starts_all + counts_all)[:, None]
    places = jnp.where(valid, ranks_got // seq_devices, slot_rows).reshape(-1)
    by_rank = (
        jnp.zeros((slot_rows, feature_width), jnp.bfloat16)
        .at[places]
        .set(incoming.reshape(-1, feature_width), mode="drop")
    )
    local_row = pack_rows - seq_index * slot_rows
    inverse = (
        jnp.zeros((slot_rows,), jnp.int32).at[local_row].set(jnp.arange(slot_rows, dtype=jnp.int32))
    )
    packed = by_rank[inverse]
    heads_local = feature_width // HEAD_DIM
    gathered = lax.all_gather(packed, "mp", axis=1, tiled=True)
    normed = layer_norm(gathered, ln_gains[0]).astype(jnp.bfloat16)
    projected = jnp.dot(
        normed, w_qkv.reshape(w_qkv.shape[0], -1), preferred_element_type=jnp.float32
    ).astype(jnp.bfloat16)
    queries = projected[:, :feature_width].reshape(slot_rows, heads_local, HEAD_DIM)
    key_rows = projected[:, feature_width : 2 * feature_width]
    value_rows = projected[:, 2 * feature_width :]
    score_scale = 1.0 / math.sqrt(HEAD_DIM)
    start_state = (
        jnp.full((heads_local, slot_rows), -jnp.inf, jnp.float32),
        jnp.zeros((heads_local, slot_rows), jnp.float32),
        jnp.zeros((slot_rows, heads_local, HEAD_DIM), jnp.float32),
    )
    carry = start_state
    piece_keys = lax.all_gather(key_rows, "seq", axis=0, tiled=True)
    piece_values = lax.all_gather(value_rows, "seq", axis=0, tiled=True)
    piece_rows = piece_keys.shape[0]
    block_rows = math.gcd(piece_rows, 512)
    piece_keys = piece_keys.reshape(piece_rows // block_rows, block_rows, heads_local, HEAD_DIM)
    piece_values = piece_values.reshape(piece_rows // block_rows, block_rows, heads_local, HEAD_DIM)

    def advance(state, block_pair):
        running_max, totals, weighted = state
        block_keys, block_values = block_pair
        scores = (
            jnp.einsum("qhd,khd->hqk", queries, block_keys, preferred_element_type=jnp.float32)
            * score_scale
        )
        new_max = jnp.maximum(running_max, jnp.max(scores, axis=2))
        factor = jnp.exp(running_max - new_max)
        expo = jnp.exp(scores - new_max[:, :, None])
        totals = totals * factor + jnp.sum(expo, axis=2)
        weighted = weighted * jnp.transpose(factor)[:, :, None] + jnp.einsum(
            "hqk,khd->qhd",
            expo.astype(jnp.bfloat16),
            block_values,
            preferred_element_type=jnp.float32,
        )
        return ((new_max, totals, weighted), None)

    carry, _ = lax.scan(advance, carry, (piece_keys, piece_values))
    running_max, totals, weighted = carry
    attended = (
        (weighted / jnp.transpose(totals)[:, :, None])
        .reshape(slot_rows, feature_width)
        .astype(jnp.bfloat16)
    )
    attn_terms = rounded(jnp.dot(attended, w_attn_out, preferred_element_type=jnp.float32))
    attn_mixed = lax.psum_scatter(
        attn_terms.astype(jnp.bfloat16), "mp", scatter_dimension=1, tiled=True
    ).astype(jnp.float32)
    first_out = (packed.astype(jnp.float32) + attn_mixed).astype(jnp.bfloat16)
    gathered_two = lax.all_gather(first_out, "mp", axis=1, tiled=True)
    normed_two = layer_norm(gathered_two, ln_gains[1]).astype(jnp.bfloat16)
    hidden = jax.nn.gelu(
        jnp.dot(normed_two, w_up, preferred_element_type=jnp.float32), approximate=False
    ).astype(jnp.bfloat16)
    mlp_terms = rounded(jnp.dot(hidden, w_down, preferred_element_type=jnp.float32))
    mlp_mixed = lax.psum_scatter(
        mlp_terms.astype(jnp.bfloat16), "mp", scatter_dimension=1, tiled=True
    ).astype(jnp.float32)
    student_rows = (first_out.astype(jnp.float32) + mlp_mixed).astype(jnp.bfloat16)
    filler = lax.dynamic_slice_in_dim(
        mask_emb, lax.axis_index("mp") * feature_width, feature_width, 0
    )
    by_rank_out = student_rows[local_row]
    everything = lax.all_gather(by_rank_out, "seq", axis=0, tiled=True)
    safe_rank = jnp.clip(global_rank, 0, seq_devices * slot_rows - 1)
    dealt_slot = safe_rank % seq_devices * slot_rows + safe_rank // seq_devices
    returned = everything[dealt_slot]
    grid_rows = jnp.where(keep_flags[:, None] == 1, returned, filler[None, :])
    grid_whole = lax.all_gather(grid_rows, "mp", axis=1, tiled=True)
    activity = lax.dot_general(
        w_dec_in, grid_whole, (((0,), (1,)), ((), ())), preferred_element_type=jnp.float32
    ).astype(jnp.bfloat16)
    channels_local = activity.shape[0]
    groups_local = channels_local // CG
    for block_id in range(BLOCKS):
        padded = with_halo(activity, (("seq", 1),), KW // 2)
        shifted = jnp.stack(
            [padded[:, tap_index : tap_index + frame_count] for tap_index in range(KW)], axis=0
        )
        shifted = shifted.reshape(KW, groups_local, CG, frame_count)
        kernel = w_conv[block_id].reshape(KW, groups_local, CG, CG)
        conv = jnp.einsum(
            "tgoi,tgif->gof", kernel, shifted, preferred_element_type=jnp.float32
        ).reshape(channels_local, frame_count)
        channel_sums, square_sums = lax.psum(
            (jnp.sum(conv, axis=0), jnp.sum(conv * conv, axis=0)), "mp"
        )
        centre = channel_sums / C
        square_mean = square_sums / C
        normal = (conv - centre) * lax.rsqrt(square_mean - centre * centre + NORM_EPSILON)
        result = jax.nn.gelu(normal, approximate=False)
        if block_id > 0:
            result = result + activity.astype(jnp.float32)
        activity = result.astype(jnp.bfloat16)
    predicted = lax.psum_scatter(
        rounded(
            lax.dot_general(
                w_dec_out, activity, (((0,), (0,)), ((), ())), preferred_element_type=jnp.float32
            )
        ).astype(jnp.bfloat16),
        "mp",
        scatter_dimension=0,
        tiled=True,
    ).astype(jnp.float32)
    masked = (1 - keep_flags).astype(jnp.float32)[None, :]
    pred_error = ((predicted - targets.astype(jnp.float32)) * masked).astype(jnp.bfloat16)
    return (student_rows, pred_error)


def solution(mesh):
    return jax.shard_map(
        local,
        mesh=mesh,
        in_specs=(
            P("seq", "mp"),
            P("seq"),
            P("seq"),
            P(),
            P(None, None, "mp"),
            P("mp", None),
            P(None, "mp"),
            P("mp", None),
            P(),
            P(None, "mp"),
            P(None, None, "mp", None),
            P("mp", None),
            P("mp", "seq"),
        ),
        out_specs=(P("seq", "mp"), P("mp", "seq")),
        check_vma=False,
    )
```

profile of v0, /device:TPU:1, one launch (start us, length us, event | category | flops | bytes accessed | tf_op | source)
XLA Modules:
  0.0 724.1 jit_solution(17021382085258005828)
XLA Ops:
  7.2 1.4 reduce_sum.126
  9.9 1.4 dynamic-update-slice
  11.3 20.0 %all-reduce = s32[32]{0:T(128)S(1)} all-reduce(s32[32]{0:T(128)S(1)} %dynamic-update-slice), channel_id=1, replica_groups=mesh['seq'=32,'mp'=8] {'seq'}, use_global_device_ids=true, to_apply=%add | all-reduce | flops 32 | bytes 256
  33.5 1.4 subtract_compare_fusion
  36.2 1.4 compare_select_fusion.2
  37.7 6.4 scatter_custom_fusion
  44.1 4.5 gather_fusion
  48.9 1.9 gather_fusion.1
  51.6 3.9 all-to-all-start
  55.6 2.9 scatter_custom_fusion.2
  60.0 4.8 all-to-all-done
  64.9 4.2 scatter_custom_fusion.1
  69.1 1.4 gather_fusion.2
  70.6 20.3 %all-gather = bf16[384,1024]{1,0:T(8,128)(2,1)S(1)} all-gather(bf16[384,128]{1,0:T(8,128)(2,1)S(1)} %gather_fusion.2), channel_id=2, replica_groups=mesh['seq'=32,'mp'=8] {'mp'}, dimensions={1}, use_global_device_ids=true | all-gather | bytes 884736 | tf_op jit(solution)/shard_map/all_gather | solution.py:98
  94.2 68.6 %all-gather.7.cloned.1.call-done = bf16[12288,128]{0,1:T(8,128)(2,1)} async-done(((bf16[384,128]{0,1:T(8,128)(2,1)}), bf16[12288,128]{0,1:T(8,128)(2,1)}) %all-gather.7.cloned.1.call-update) | async-done | bytes 3145744 | tf_op jit(solution)/shard_map/all_gather | solution.py:113
  162.8 3.2 copy.81
  166.0 2.7 copy.55
  168.7 75.5 %all-gather.9.cloned.1.call-done = bf16[12288,128]{0,1:T(8,128)(2,1)} async-done(((bf16[384,128]{0,1:T(8,128)(2,1)}), bf16[12288,128]{0,1:T(8,128)(2,1)}) %all-gather.9.cloned.1.call-update) | async-done | bytes 3145744 | tf_op jit(solution)/shard_map/all_gather | solution.py:114
  244.2 3.2 copy.82
  247.4 2.8 copy.56
  250.2 70.5 %while.15 = (s32[]{:T(128)}, f32[2,384]{1,0:T(2,128)S(1)}, f32[2,384]{1,0:T(2,128)S(1)}, f32[384,2,64]{0,2,1:T(8,128)S(1)}, bf16[24,512,2,64]{1,3,2,0:T(8,128)(2...) while((s32[]{:T(128)}, f32[2,384]{1,0:T(2,128)S(1)}, ...), condition=%wide.region_12.13_spmd.clone, body=%wide.region_9.12_spmd.clone.sunk | while | flops 103174656 | bytes 5522537 | solution.py:139
  250.2 1.4 bitcast_reduce_fusion.6
  253.1 1.3 bitcast_reduce_fusion.6
  259.0 1.3 bitcast_reduce_fusion.6
  261.9 1.3 bitcast_reduce_fusion.6
  264.9 1.3 bitcast_reduce_fusion.6
  267.8 1.3 bitcast_reduce_fusion.6
  270.7 1.3 bitcast_reduce_fusion.6
  273.7 1.3 bitcast_reduce_fusion.6
  276.6 1.3 bitcast_reduce_fusion.6
  279.5 1.3 bitcast_reduce_fusion.6
  285.4 1.3 bitcast_reduce_fusion.6
  288.4 1.3 bitcast_reduce_fusion.6
  291.3 1.3 bitcast_reduce_fusion.6
  294.2 1.3 bitcast_reduce_fusion.6
  303.0 1.3 bitcast_reduce_fusion.6
  306.0 1.3 bitcast_reduce_fusion.6
  308.9 1.3 bitcast_reduce_fusion.6
  311.8 1.3 bitcast_reduce_fusion.6
  322.3 34.9 %reduce-scatter.10.cloned.1.call-done = bf16[128,384]{1,0:T(8,128)(2,1)} async-done(((bf16[1024,384]{1,0:T(8,128)(2,1)}), bf16[128,384]{1,0:T(8,128)(2,1)}) %reduce-scatter.10.cloned.1.call-update) | async-done | bytes 98320
  358.3 15.8 %all_gather.25 = bf16[384,1024]{1,0:T(8,128)(2,1)S(1)} all-gather(bf16[384,128]{1,0:T(8,128)(2,1)S(1)} %add_convert_fusion.1), channel_id=1, replica_groups=mesh['seq'=32,'mp'=8] {'mp'}, dimensions={1}, use_global_device_ids=true | all-gather | bytes 884736 | tf_op jit(solution)/shard_map/all_gather | solution.py:151
  374.6 4.0 convolution_convert_fusion.2
  379.8 32.8 %reduce-scatter.12.cloned.1.call-done = bf16[128,384]{1,0:T(8,128)(2,1)} async-done(((bf16[1024,384]{1,0:T(8,128)(2,1)}), bf16[128,384]{1,0:T(8,128)(2,1)}) %reduce-scatter.12.cloned.1.call-update) | async-done | bytes 98320
  413.6 1.9 gather_fusion.3
  416.6 75.7 %all-gather.13.cloned.1.call-done = bf16[12288,128]{1,0:T(8,128)(2,1)} async-done(((bf16[384,128]{1,0:T(8,128)(2,1)}), bf16[12288,128]{1,0:T(8,128)(2,1)}) %all-gather.13.cloned.1.call-update) | async-done | bytes 3145744 | tf_op jit(solution)/shard_map/all_gather | solution.py:165
  492.3 4.8 gather_fusion.4
  498.2 31.4 %all-gather.11.cloned.1.call-done = bf16[1152,1024]{1,0:T(8,128)(2,1)} async-done(((bf16[1152,128]{1,0:T(8,128)(2,1)}), bf16[1152,1024]{1,0:T(8,128)(2,1)}) %all-gather.11.cloned.1.call-update) | async-done | bytes 2359312 | tf_op jit(solution)/shard_map/all_gather | solution.py:170
  529.6 2.5 convolution_convert_fusion.1
  532.2 3.2 collective-permute-start
  536.8 3.1 collective-permute-done.1
  541.1 22.0 %all-reduce.4 = (f32[1152]{0:T(1024)S(1)}, f32[1152]{0:T(1024)S(1)}) all-reduce(f32[1152]{0:T(1024)S(1)} %get-tuple-element.189, f32[1152]{0:T(1024)S(1)} %bitcast_reduce_fusion.4), channel_id=1, replica_groups=mesh['seq'=32,'mp'=8] {'mp'}, use_global_device_ids=true, to_apply=%region_20.21 | all-reduce | flops 2304 | bytes 18432 | tf_op jit(solution)/shard_map/psum | solution.py:186
  564.2 3.2 collective-permute-start.2
  568.8 4.0 collective-permute-done.3
  575.0 24.7 %all-reduce.3 = (f32[1152]{0:T(1024)S(1)}, f32[1152]{0:T(1024)S(1)}) all-reduce(f32[1152]{0:T(1024)S(1)} %get-tuple-element.191, f32[1152]{0:T(1024)S(1)} %bitcast_reduce_fusion.3), channel_id=1, replica_groups=mesh['seq'=32,'mp'=8] {'mp'}, use_global_device_ids=true, to_apply=%region_24.25 | all-reduce | flops 2304 | bytes 18432 | tf_op jit(solution)/shard_map/psum | solution.py:186
  599.7 2.0 fusion.58
  601.7 4.6 collective-permute-start.4
  607.8 3.4 collective-permute-done.5
  613.3 25.0 %all-reduce.2 = (f32[1152]{0:T(1024)S(1)}, f32[1152]{0:T(1024)S(1)}) all-reduce(f32[1152]{0:T(1024)S(1)} %get-tuple-element.193, f32[1152]{0:T(1024)S(1)} %bitcast_reduce_fusion.2), channel_id=1, replica_groups=mesh['seq'=32,'mp'=8] {'mp'}, use_global_device_ids=true, to_apply=%region_28.29 | all-reduce | flops 2304 | bytes 18432 | tf_op jit(solution)/shard_map/psum | solution.py:186
  639.4 3.6 collective-permute-start.6
  644.5 3.1 collective-permute-done.7
  649.8 25.0 %all-reduce.1 = (f32[1152]{0:T(1024)S(1)}, f32[1152]{0:T(1024)S(1)}) all-reduce(f32[1152]{0:T(1024)S(1)} %get-tuple-element.195, f32[1152]{0:T(1024)S(1)} %bitcast_reduce_fusion.1), channel_id=1, replica_groups=mesh['seq'=32,'mp'=8] {'mp'}, use_global_device_ids=true, to_apply=%region_32.33 | all-reduce | flops 2304 | bytes 18432 | tf_op jit(solution)/shard_map/psum | solution.py:186
  675.8 1.7 fusion.15
  677.6 2.6 copy.79
  681.3 33.4 %reduce-scatter.14.cloned.1.call-done = bf16[128,1152]{1,0:T(8,128)(2,1)} async-done(((bf16[1024,1152]{1,0:T(8,128)(2,1)}), bf16[128,1152]{1,0:T(8,128)(2,1)}) %reduce-scatter.14.cloned.1.call-update) | async-done | bytes 294928
  (290 shorter events, 83.4 us)
Async XLA Ops:
  7.2 367.4 %copy-start = (bf16[512,1024]{1,0:T(8,128)(2,1)S(1)}, bf16[512,1024]{1,0:T(8,128)(2,1)}, u32[]{:S(2)}) copy-start(bf16[512,1024]{1,0:T(8,128)(2,1)} %param.22) | copy-start | bytes 3145732
  44.1 4.7 copy-start.11
  44.1 4.7 copy-start.1
  48.6 10.2 %copy-start.3 = (bf16[1024,3,128]{2,0,1:T(8,128)(2,1)S(1)}, bf16[1024,3,128]{2,0,1:T(8,128)(2,1)}, u32[]{:S(2)}) copy-start(bf16[1024,3,128]{2,0,1:T(8,128)(2,1)} %param.19) | copy-start | bytes 2359300
  50.8 9.3 %copy-start.10 = (f32[2,1024]{1,0:T(2,128)S(1)}, f32[2,1024]{1,0:T(2,128)}, u32[]{:S(2)}) copy-start(f32[2,1024]{1,0:T(2,128)} %param.18) | copy-start | bytes 24580
  51.6 13.3 %all-to-all-start = ((bf16[32,24,128]{2,1,0:T(8,128)(2,1)}), bf16[32,24,128]{2,1,0:T(8,128)(2,1)S(1)}, u32[]{:S(2)}, u32[]{:S(2)}) async-start(bf16[32,24,128]{2,1,0:T(8,128)(2,1)} %broadcast_select_fusion.2), calls=%async_computation | async-start | bytes 393216 | tf_op jit(solution)/shard_map/all_to_all | solution.py:82
  55.5 107.3 %all-gather.7.cloned.1.call-start = ((), (), s32[]{:S(2)}) async-start(), calls=%async_computation.4 | async-start | bytes 3244032 | tf_op jit(solution)/shard_map/all_gather | solution.py:113
  69.1 22.3 %copy-start.4 = (bf16[1024,3,128]{0,2,1:T(8,128)(2,1)S(1)}, bf16[1024,3,128]{0,2,1:T(8,128)(2,1)}, u32[]{:S(2)}) copy-start(bf16[1024,3,128]{0,2,1:T(8,128)(2,1)} %copy.54) | copy-start | bytes 2359300
  92.9 151.3 %all-gather.9.cloned.1.call-start = ((), (), s32[]{:S(2)}) async-start(), calls=%async_computation.5 | async-start | bytes 3244032 | tf_op jit(solution)/shard_map/all_gather | solution.py:114
  93.6 263.6 %reduce-scatter.10.cloned.1.call-start = ((), (), s32[]{:S(2)}) async-start(), calls=%async_computation.8 | async-start | bytes 884736
  250.2 70.5 %copy-start.7 = (bf16[128,1024]{1,0:T(8,128)(2,1)S(1)}, bf16[128,1024]{1,0:T(8,128)(2,1)}, u32[]{:S(2)}) copy-start(bf16[128,1024]{1,0:T(8,128)(2,1)} %param.20) | copy-start | bytes 786436
  322.2 90.3 %reduce-scatter.12.cloned.1.call-start = ((), (), s32[]{:S(2)}) async-start(), calls=%async_computation.9 | async-start | bytes 884736
  378.5 38.0 %copy-start.9 = (s32[1152]{0:T(1024)S(1)}, s32[1152]{0:T(1024)}, u32[]{:S(2)}) copy-start(s32[1152]{0:T(1024)} %param.16) | copy-start | bytes 13828
  379.7 112.6 %all-gather.13.cloned.1.call-start = ((), (), s32[]{:S(2)}) async-start(), calls=%async_computation.7 | async-start | bytes 3244032 | tf_op jit(solution)/shard_map/all_gather | solution.py:165
  413.6 83.5 %copy-start.2 = (bf16[384,128]{1,0:T(8,128)(2,1)}, bf16[384,128]{1,0:T(8,128)(2,1)S(1)}, u32[]{:S(2)}) copy-start(bf16[384,128]{1,0:T(8,128)(2,1)S(1)} %add_convert_fusion) | copy-start | bytes 294916
  415.5 114.0 %all-gather.11.cloned.1.call-start = ((), (), s32[]{:S(2)}) async-start(), calls=%async_computation.6 | async-start | bytes 2654208 | tf_op jit(solution)/shard_map/all_gather | solution.py:170
  416.6 113.0 %copy-start.8 = (bf16[1024,96]{0,1:T(8,128)(2,1)S(1)}, bf16[1024,96]{0,1:T(8,128)(2,1)}, u32[]{:S(2)}) copy-start(bf16[1024,96]{0,1:T(8,128)(2,1)} %param.24) | copy-start | bytes 589828
  498.1 38.6 %copy-start.5 = (bf16[4,7,96,48]{2,3,1,0:T(8,128)(2,1)S(1)}, bf16[4,7,96,48]{2,3,1,0:T(8,128)(2,1)}, u32[]{:S(2)}) copy-start(bf16[4,7,96,48]{2,3,1,0:T(8,128)(2,1)} %param.25) | copy-start | bytes 774148
  498.1 216.6 %reduce-scatter.14.cloned.1.call-start = ((), (), s32[]{:S(2)}) async-start(), calls=%async_computation.10 | async-start | bytes 2654208
  532.2 4.6 collective-permute-start
  535.3 4.6 collective-permute-start.1
  564.2 4.6 collective-permute-start.2
  567.4 5.4 collective-permute-start.3
  601.7 6.0 collective-permute-start.4
  606.3 4.9 collective-permute-start.5
  639.4 5.1 collective-permute-start.6
  643.0 4.6 collective-permute-start.7
  680.1 1.0 copy-start.6
Sparse Core Ops, SparseCore 0:
  93.0 69.7 all-gather.6
  165.9 78.2 all-gather.8
  322.4 34.7 reduce-scatter.9
  379.8 32.6 reduce-scatter.11
  415.7 76.6 all-gather.12
  498.2 31.3 all-gather.10
  680.3 34.4 reduce-scatter.13
where the time goes:
time: 735 us; the launch traced here: 724 us
  waiting for transfers between devices  372 us (51%)
  blocking collectives  153 us (21%)
  matrix products  74.1 us (10%)
  local copies, waits for them, and re-layouts  58.3 us (8%)
  other arithmetic  26.4 us (4%)
  starting transfers between devices  24.5 us (3%)
  between operations  15.2 us (2%)
    unnamed x10, waiting for transfers between devices  102 us
    psum x4, blocking collectives, local(): lax.psum((jnp.sum(conv, axis=0), jnp.sum(conv * conv, axis=0)), 'mp')  96.7 us
    all_gather x1, waiting for transfers between devices, local(): everything = lax.all_gather(by_rank_out, 'seq', axis=0, tiled=True)  75.7 us
    all_gather x1, waiting for transfers between devices, local(): piece_values = lax.all_gather(value_rows, 'seq', axis=0, tiled=True)  75.5 us
    all_gather x1, waiting for transfers between devices, local(): piece_keys = lax.all_gather(key_rows, 'seq', axis=0, tiled=True)  68.6 us
    dot_general x24, matrix products, advance(): jnp.einsum('qhd,khd->hqk', queries, block_keys, preferred_element_type=jn...  32 us
    all_gather x1, waiting for transfers between devices, local(): grid_whole = lax.all_gather(grid_rows, 'mp', axis=1, tiled=True)  31.4 us
    dot_general x24, matrix products, advance(): jnp.einsum('hqk,khd->qhd', expo.astype(jnp.bfloat16), block_values, prefe...  30.9 us
  transfers between devices with their start and end apart: 16, of which 12 were waited for; matrix products, arithmetic and copies ran while one was open for 2% of the time, Pallas kernels for 0%

commit v1 on v0

--- a/solution.py
+++ b/solution.py
@@ -26,6 +26,20 @@
         high = lax.ppermute(lax.slice_in_dim(block, 0, width, axis=dim), axis, backward)
         block = jnp.concatenate([low, block, high], axis=dim)
     return block
+
+
+def gather_all(values, axis):
+    count = lax.axis_size(axis)
+    spread = jnp.broadcast_to(values[None], (count,) + values.shape)
+    return lax.all_to_all(spread, axis, 0, 0, tiled=True)
+
+
+def sum_scatter(pieces, axis, dim):
+    count = lax.axis_size(axis)
+    shape = pieces.shape
+    split = pieces.reshape(shape[:dim] + (count, shape[dim] // count) + shape[dim + 1 :])
+    moved = lax.all_to_all(split, axis, dim, dim, tiled=True)
+    return jnp.sum(moved.astype(jnp.float32), axis=dim)
 
 
 def layer_norm(values, gain):
@@ -61,7 +75,7 @@
     seq_index = lax.axis_index("seq")
     capacity = (2 * slot_rows + seq_devices - 1) // seq_devices
     kept_count = jnp.sum(keep_flags)
-    counts_all = lax.all_gather(kept_count[None], "seq", axis=0, tiled=True)
+    counts_all = gather_all(kept_count[None], "seq").reshape(seq_devices)
     starts_all = jnp.cumsum(counts_all) - counts_all
     kept_before = starts_all[seq_index]
     local_rank = jnp.cumsum(keep_flags) - keep_flags
@@ -71,7 +85,6 @@
         .at[jnp.where(keep_flags == 1, local_rank, frame_count)]
         .set(frame_index, mode="drop")
     )
-    global_rank = kept_before + local_rank
     slot_steps = jnp.arange(capacity, dtype=jnp.int32)[None, :] * seq_devices
     owners = jnp.arange(seq_devices, dtype=jnp.int32)
     first_sent = kept_before + (owners - kept_before) % seq_devices
@@ -101,8 +114,6 @@
         normed, w_qkv.reshape(w_qkv.shape[0], -1), preferred_element_type=jnp.float32
     ).astype(jnp.bfloat16)
     queries = projected[:, :feature_width].reshape(slot_rows, heads_local, HEAD_DIM)
-    key_rows = projected[:, feature_width : 2 * feature_width]
-    value_rows = projected[:, 2 * feature_width :]
     score_scale = 1.0 / math.sqrt(HEAD_DIM)
     start_state = (
         jnp.full((heads_local, slot_rows), -jnp.inf, jnp.float32),
@@ -110,8 +121,9 @@
         jnp.zeros((slot_rows, heads_local, HEAD_DIM), jnp.float32),
     )
     carry = start_state
-    piece_keys = lax.all_gather(key_rows, "seq", axis=0, tiled=True)
-    piece_values = lax.all_gather(value_rows, "seq", axis=0, tiled=True)
+    key_value = lax.all_gather(projected[:, feature_width:], "seq", axis=0, tiled=True)
+    piece_keys = key_value[:, :feature_width]
+    piece_values = key_value[:, feature_width:]
     piece_rows = piece_keys.shape[0]
     block_rows = math.gcd(piece_rows, 512)
     piece_keys = piece_keys.reshape(piece_rows // block_rows, block_rows, heads_local, HEAD_DIM)
@@ -144,9 +156,7 @@
         .astype(jnp.bfloat16)
     )
     attn_terms = rounded(jnp.dot(attended, w_attn_out, preferred_element_type=jnp.float32))
-    attn_mixed = lax.psum_scatter(
-        attn_terms.astype(jnp.bfloat16), "mp", scatter_dimension=1, tiled=True
-    ).astype(jnp.float32)
+    attn_mixed = sum_scatter(attn_terms.astype(jnp.bfloat16), "mp", 1)
     first_out = (packed.astype(jnp.float32) + attn_mixed).astype(jnp.bfloat16)
     gathered_two = lax.all_gather(first_out, "mp", axis=1, tiled=True)
     normed_two = layer_norm(gathered_two, ln_gains[1]).astype(jnp.bfloat16)
@@ -154,18 +164,18 @@
         jnp.dot(normed_two, w_up, preferred_element_type=jnp.float32), approximate=False
     ).astype(jnp.bfloat16)
     mlp_terms = rounded(jnp.dot(hidden, w_down, preferred_element_type=jnp.float32))
-    mlp_mixed = lax.psum_scatter(
-        mlp_terms.astype(jnp.bfloat16), "mp", scatter_dimension=1, tiled=True
-    ).astype(jnp.float32)
+    mlp_mixed = sum_scatter(mlp_terms.astype(jnp.bfloat16), "mp", 1)
     student_rows = (first_out.astype(jnp.float32) + mlp_mixed).astype(jnp.bfloat16)
     filler = lax.dynamic_slice_in_dim(
         mask_emb, lax.axis_index("mp") * feature_width, feature_width, 0
     )
     by_rank_out = student_rows[local_row]
-    everything = lax.all_gather(by_rank_out, "seq", axis=0, tiled=True)
-    safe_rank = jnp.clip(global_rank, 0, seq_devices * slot_rows - 1)
-    dealt_slot = safe_rank % seq_devices * slot_rows + safe_rank // seq_devices
-    returned = everything[dealt_slot]
+    back_out = by_rank_out[jnp.clip(places, 0, slot_rows - 1)].reshape(
+        seq_devices, capacity, feature_width
+    )
+    back_in = lax.all_to_all(back_out, "seq", 0, 0, tiled=True).reshape(-1, feature_width)
+    back_index = ((kept_before + local_rank) % seq_devices) * capacity + local_rank // seq_devices
+    returned = back_in[jnp.clip(back_index, 0, seq_devices * capacity - 1)]
     grid_rows = jnp.where(keep_flags[:, None] == 1, returned, filler[None, :])
     grid_whole = lax.all_gather(grid_rows, "mp", axis=1, tiled=True)
     activity = lax.dot_general(
@@ -183,9 +193,10 @@
         conv = jnp.einsum(
             "tgoi,tgif->gof", kernel, shifted, preferred_element_type=jnp.float32
         ).reshape(channels_local, frame_count)
-        channel_sums, square_sums = lax.psum(
-            (jnp.sum(conv, axis=0), jnp.sum(conv * conv, axis=0)), "mp"
-        )
+        stats = jnp.stack([jnp.sum(conv, axis=0), jnp.sum(conv * conv, axis=0)], axis=0)
+        stats = jnp.sum(gather_all(stats, "mp"), axis=0)
+        channel_sums = stats[0]
+        square_sums = stats[1]
         centre = channel_sums / C
         square_mean = square_sums / C
         normal = (conv - centre) * lax.rsqrt(square_mean - centre * centre + NORM_EPSILON)
@@ -193,16 +204,15 @@
         if block_id > 0:
             result = result + activity.astype(jnp.float32)
         activity = result.astype(jnp.bfloat16)
-    predicted = lax.psum_scatter(
+    predicted = sum_scatter(
         rounded(
             lax.dot_general(
                 w_dec_out, activity, (((0,), (0,)), ((), ())), preferred_element_type=jnp.float32
             )
         ).astype(jnp.bfloat16),
         "mp",
-        scatter_dimension=0,
-        tiled=True,
-    ).astype(jnp.float32)
+        0,
+    )
     masked = (1 - keep_flags).astype(jnp.float32)[None, :]
     pred_error = ((predicted - targets.astype(jnp.float32)) * masked).astype(jnp.bfloat16)
     return (student_rows, pred_error)

time: 735 us -> 508 us (0.69)
  waiting for transfers between devices: 372 us -> 183 us
  blocking collectives: 153 us -> 89.3 us
  starting transfers between devices: 24.5 us -> 56.8 us
    all_gather x3 -> x1, waiting for transfers between devices: 220 us -> 82.8 us  [local(): lax.all_gather(projected[:, feature_width:], 'seq', axis=0, tiled=True)]
    unnamed x10 -> x2, waiting for transfers between devices: 102 us -> 0.03 us
    psum x4 -> x0, blocking collectives: 96.7 us -> none  [local(): lax.psum((jnp.sum(conv, axis=0), jnp.sum(conv * conv, axis=0)), 'mp')]
    all_to_all x0 -> x5, blocking collectives: none -> 57.9 us  [the longest x4 38.4 us: gather_all(): return lax.all_to_all(spread, axis, 0, 0, tiled=True)]
    all_to_all x0 -> x4, waiting for transfers between devices: none -> 51.8 us  [the longest x2 40.3 us: sum_scatter(): moved = lax.all_to_all(split, axis, dim, dim, tiled=True)]
    all_to_all x0 -> x4, starting transfers between devices: none -> 30.5 us  [the longest x1 11.9 us: gather_all(): return lax.all_to_all(spread, axis, 0, 0, tiled=True)]
    unnamed x1 -> x0, blocking collectives: 20 us -> none
    unnamed x61 -> x56, local copies, waits for them, and re-layouts: 26.3 us -> 12.2 us
  transfers between devices with their start and end apart: 16 -> 15, of which waited for: 12 -> 11; matrix products, arithmetic and copies ran while one was open for 2% -> 2% of each run, Pallas kernels for 0% -> 0%
where the time goes in v1:
time: 508 us; the launch traced here: 500 us
  waiting for transfers between devices  183 us (36%)
  blocking collectives  89.3 us (18%)
  matrix products  73.1 us (14%)
  starting transfers between devices  56.8 us (11%)
  local copies, waits for them, and re-layouts  52.8 us (10%)
  other arithmetic  28.6 us (6%)
  between operations  15.5 us (3%)
    all_gather x1, waiting for transfers between devices, local(): lax.all_gather(projected[:, feature_width:], 'seq', axis=0, tiled=True)  82.8 us
    all_to_all x2, waiting for transfers between devices, sum_scatter(): moved = lax.all_to_all(split, axis, dim, dim, tiled=True)  40.3 us
    all_to_all x4, blocking collectives, gather_all(): return lax.all_to_all(spread, axis, 0, 0, tiled=True)  38.4 us
    dot_general x24, matrix products, advance(): jnp.einsum('qhd,khd->hqk', queries, block_keys, preferred_element_type=jn...  32 us
    dot_general x24, matrix products, advance(): jnp.einsum('hqk,khd->qhd', expo.astype(jnp.bfloat16), block_values, prefe...  30.9 us
    all_gather x1, waiting for transfers between devices, local(): grid_whole = lax.all_gather(grid_rows, 'mp', axis=1, tiled=True)  26.9 us
    all_to_all x1, blocking collectives, sum_scatter(): moved = lax.all_to_all(split, axis, dim, dim, tiled=True)  19.5 us
    all_gather x1, blocking collectives, local(): gathered = lax.all_gather(packed, 'mp', axis=1, tiled=True)  17.3 us
  transfers between devices with their start and end apart: 15, of which 11 were waited for; matrix products, arithmetic and copies ran while one was open for 2% of the time, Pallas kernels for 0%

profile of v1, /device:TPU:1, one launch (start us, length us, event | category | flops | bytes accessed | tf_op | source)
XLA Modules:
  0.0 499.9 jit_solution(8805742650085946966)
XLA Ops:
  7.2 1.4 reduce_sum.189
  9.9 11.9 %all-to-all-start = ((s32[32,1,1]{2,1,0:T(1,128)}), s32[32,1,1]{2,1,0:T(1,128)S(1)}, u32[]{:S(2)}, u32[]{:S(2)}) async-start(s32[32,1,1]{2,1,0:T(1,128)} %broadcast_in_dim.65), calls=%async_computation | async-start | bytes 32768 | tf_op jit(solution)/shard_map/all_to_all | solution.py:34
  23.6 2.9 scatter_custom_fusion.2
  27.3 3.0 all-to-all-done
  33.1 1.4 subtract_compare_fusion
  34.6 1.4 compare_select_fusion.2
  36.1 6.4 %scatter_custom_fusion = s32[1152]{0:T(1024)S(1)} fusion(s32[1152]{0:T(1024)S(1)} %get-tuple-element.201, s32[1152]{0:T(1024)S(1)} %iota.22, s32[]{:T(128)} %constant.66.clone.1), kind=kCustom, calls=%fused_computation.431 | custom fusion | bytes 4612 | tf_op jit(solution)/shard_map/scatter | solution.py:86
  42.5 4.5 gather_fusion
  47.2 1.9 gather_fusion.1
  49.9 6.3 %all-to-all-start.1 = ((bf16[32,24,128]{2,1,0:T(8,128)(2,1)}), bf16[32,24,128]{2,1,0:T(8,128)(2,1)S(1)}, u32[]{:S(2)}, u32[]{:S(2)}) async-start(bf16[32,24,128]{2,1,0:T(8,128)(2,1)} %broadcast_select_fusion.2), calls=%async_computation.1 | async-start | bytes 393216 | tf_op jit(solution)/shard_map/all_to_all | solution.py:95
  57.8 7.8 %all-to-all-done.1 = bf16[32,24,128]{2,1,0:T(8,128)(2,1)S(1)} async-done(((bf16[32,24,128]{2,1,0:T(8,128)(2,1)}), bf16[32,24,128]{2,1,0:T(8,128)(2,1)S(1)}, u32[]{:S(2)}, u32[]{:S(2)}) %all-to-all-start.1) | async-done | bytes 196640 | tf_op jit(solution)/shard_map/all_to_all | solution.py:95
  65.6 4.2 scatter_custom_fusion.1
  69.9 1.4 gather_fusion.2
  71.3 17.3 %all-gather = bf16[384,1024]{1,0:T(8,128)(2,1)S(1)} all-gather(bf16[384,128]{1,0:T(8,128)(2,1)S(1)} %gather_fusion.2), channel_id=2, replica_groups=mesh['seq'=32,'mp'=8] {'mp'}, dimensions={1}, use_global_device_ids=true | all-gather | bytes 884736 | tf_op jit(solution)/shard_map/all_gather | solution.py:111
  90.7 82.8 %all-gather.4.cloned.1.call-done = bf16[12288,256]{0,1:T(8,128)(2,1)} async-done(((bf16[384,256]{0,1:T(8,128)(2,1)}), bf16[12288,256]{0,1:T(8,128)(2,1)}) %all-gather.4.cloned.1.call-update) | async-done | bytes 6291472 | tf_op jit(solution)/shard_map/all_gather | solution.py:124
  173.6 3.2 fusion.243
  178.1 2.7 copy.117
  182.1 2.8 copy.118
  184.9 70.5 %while.15 = (s32[]{:T(128)}, f32[2,384]{1,0:T(2,128)S(1)}, f32[2,384]{1,0:T(2,128)S(1)}, f32[384,2,64]{0,2,1:T(8,128)S(1)}, bf16[24,512,2,64]{1,3,2,0:T(8,128)(2...) while((s32[]{:T(128)}, f32[2,384]{1,0:T(2,128)S(1)}, ...), condition=%wide.region_12.13_spmd.clone, body=%wide.region_9.12_spmd.clone.sunk | while | flops 103174656 | bytes 5522537 | solution.py:151
  184.9 1.4 bitcast_reduce_fusion.6
  187.9 1.3 bitcast_reduce_fusion.6
  190.8 1.3 bitcast_reduce_fusion.6
  193.8 1.3 bitcast_reduce_fusion.6
  196.7 1.3 bitcast_reduce_fusion.6
  199.6 1.3 bitcast_reduce_fusion.6
  202.6 1.3 bitcast_reduce_fusion.6
  205.5 1.3 bitcast_reduce_fusion.6
  208.4 1.3 bitcast_reduce_fusion.6
  211.4 1.3 bitcast_reduce_fusion.6
  214.3 1.3 bitcast_reduce_fusion.6
  217.2 1.3 bitcast_reduce_fusion.6
  220.2 1.3 bitcast_reduce_fusion.6
  223.1 1.3 bitcast_reduce_fusion.6
  226.0 1.3 bitcast_reduce_fusion.6
  229.0 1.3 bitcast_reduce_fusion.6
  240.7 1.3 bitcast_reduce_fusion.6
  256.0 19.5 %all_to_all.54 = bf16[384,8,128]{2,0,1:T(8,128)(2,1)S(1)} all-to-all(bf16[384,8,128]{2,0,1:T(8,128)(2,1)S(1)} %copy_bitcast_fusion.2), channel_id=1, replica_groups=mesh['seq'=32,'mp'=8] {'mp'}, dimensions={1} | all-to-all | bytes 1572864 | tf_op jit(solution)/shard_map/all_to_all | solution.py:41
  275.6 14.1 %all_gather.14 = bf16[384,1024]{1,0:T(8,128)(2,1)S(1)} all-gather(bf16[384,128]{1,0:T(8,128)(2,1)S(1)} %add_convert_fusion.1), channel_id=1, replica_groups=mesh['seq'=32,'mp'=8] {'mp'}, dimensions={1}, use_global_device_ids=true | all-gather | bytes 884736 | tf_op jit(solution)/shard_map/all_gather | solution.py:161
  290.2 4.0 convolution_convert_fusion.2
  295.2 4.3 all-to-all-start.3
  299.5 12.1 %all-to-all-done.3 = bf16[384,8,128]{2,0,1:T(8,128)(2,1)S(1)} async-done(((bf16[384,8,128]{2,0,1:T(8,128)(2,1)}), bf16[384,8,128]{2,0,1:T(8,128)(2,1)S(1)}, u32[]{:S(2)}, u32[]{:S(2)}) %all-to-all-start.3) | async-done | bytes 786464 | tf_op jit(solution)/shard_map/all_to_all | solution.py:41
  311.8 1.4 gather_fusion.3
  313.3 2.5 gather_fusion.4
  315.8 9.9 %all-to-all-start.4 = ((bf16[32,24,128]{2,1,0:T(8,128)(2,1)}), bf16[32,24,128]{2,1,0:T(8,128)(2,1)S(1)}, u32[]{:S(2)}, u32[]{:S(2)}) async-start(bf16[32,24,128]{2,1,0:T(8,128)(2,1)} %bitcast.12), calls=%async_computation.4 | async-start | bytes 393216 | tf_op jit(solution)/shard_map/all_to_all | solution.py:176
  326.6 8.6 %all-to-all-done.4 = bf16[32,24,128]{2,1,0:T(8,128)(2,1)S(1)} async-done(((bf16[32,24,128]{2,1,0:T(8,128)(2,1)}), bf16[32,24,128]{2,1,0:T(8,128)(2,1)S(1)}, u32[]{:S(2)}, u32[]{:S(2)}) %all-to-all-start.4) | async-done | bytes 196640 | tf_op jit(solution)/shard_map/all_to_all | solution.py:176
  335.1 2.9 gather_fusion.5
  339.0 26.9 %all-gather.6.cloned.1.call-done = bf16[1152,1024]{1,0:T(8,128)(2,1)} async-done(((bf16[1152,128]{1,0:T(8,128)(2,1)}), bf16[1152,1024]{1,0:T(8,128)(2,1)}) %all-gather.6.cloned.1.call-update) | async-done | bytes 2359312 | tf_op jit(solution)/shard_map/all_gather | solution.py:180
  365.9 2.5 convolution_convert_fusion.1
  368.5 3.2 collective-permute-start
  373.2 3.1 collective-permute-done.1
  377.5 10.3 %all_to_all.55 = f32[8,2,1152]{2,1,0:T(2,128)S(1)} all-to-all(f32[8,2,1152]{2,1,0:T(2,128)S(1)} %broadcast_in_dim.79), channel_id=1, replica_groups=mesh['seq'=32,'mp'=8] {'mp'}, dimensions={0} | all-to-all | bytes 147456 | tf_op jit(solution)/shard_map/all_to_all | solution.py:34
  389.0 3.2 collective-permute-start.2
  393.6 3.7 collective-permute-done.3
  399.5 9.4 %all_to_all.56 = f32[8,2,1152]{2,1,0:T(2,128)S(1)} all-to-all(f32[8,2,1152]{2,1,0:T(2,128)S(1)} %broadcast_in_dim.80), channel_id=1, replica_groups=mesh['seq'=32,'mp'=8] {'mp'}, dimensions={0} | all-to-all | bytes 147456 | tf_op jit(solution)/shard_map/all_to_all | solution.py:34
  409.0 2.0 fusion.58
  411.1 4.8 collective-permute-start.4
  417.4 3.4 collective-permute-done.5
  423.0 9.2 %all_to_all.57 = f32[8,2,1152]{2,1,0:T(2,128)S(1)} all-to-all(f32[8,2,1152]{2,1,0:T(2,128)S(1)} %broadcast_in_dim.134), channel_id=1, replica_groups=mesh['seq'=32,'mp'=8] {'mp'}, dimensions={0} | all-to-all | bytes 147456 | tf_op jit(solution)/shard_map/all_to_all | solution.py:34
  433.4 3.6 collective-permute-start.6
  438.5 3.1 collective-permute-done.7
  443.9 9.5 %all_to_all.58 = f32[8,2,1152]{2,1,0:T(2,128)S(1)} all-to-all(f32[8,2,1152]{2,1,0:T(2,128)S(1)} %broadcast_in_dim.135), channel_id=1, replica_groups=mesh['seq'=32,'mp'=8] {'mp'}, dimensions={0} | all-to-all | bytes 147456 | tf_op jit(solution)/shard_map/all_to_all | solution.py:34
  455.2 1.8 copy_bitcast_fusion
  457.1 4.4 all-to-all-start.9
  462.4 28.1 %all-to-all-done.9 = bf16[8,128,1152]{1,2,0:T(8,128)(2,1)S(1)} async-done(((bf16[8,128,1152]{1,2,0:T(8,128)(2,1)}), bf16[8,128,1152]{1,2,0:T(8,128)(2,1)S(1)}, u32[]{:S(2)}, u32[]{:S(2)}) %all-to-all-start.9) | async-done | bytes 2359328 | tf_op jit(solution)/shard_map/all_to_all | solution.py:41
  (311 shorter events, 85.6 us)
Async XLA Ops:
  7.2 283.0 %copy-start = (bf16[512,1024]{1,0:T(8,128)(2,1)S(1)}, bf16[512,1024]{1,0:T(8,128)(2,1)}, u32[]{:S(2)}) copy-start(bf16[512,1024]{1,0:T(8,128)(2,1)} %param.22) | copy-start | bytes 3145732
  9.9 20.5 %all-to-all-start = ((s32[32,1,1]{2,1,0:T(1,128)}), s32[32,1,1]{2,1,0:T(1,128)S(1)}, u32[]{:S(2)}, u32[]{:S(2)}) async-start(s32[32,1,1]{2,1,0:T(1,128)} %broadcast_in_dim.65), calls=%async_computation | async-start | bytes 32768 | tf_op jit(solution)/shard_map/all_to_all | solution.py:34
  42.5 4.7 copy-start.2
  47.0 9.3 %copy-start.6 = (bf16[1024,3,128]{2,0,1:T(8,128)(2,1)S(1)}, bf16[1024,3,128]{2,0,1:T(8,128)(2,1)}, u32[]{:S(2)}) copy-start(bf16[1024,3,128]{2,0,1:T(8,128)(2,1)} %param.19) | copy-start | bytes 2359300
  49.9 15.7 %all-to-all-start.1 = ((bf16[32,24,128]{2,1,0:T(8,128)(2,1)}), bf16[32,24,128]{2,1,0:T(8,128)(2,1)S(1)}, u32[]{:S(2)}, u32[]{:S(2)}) async-start(bf16[32,24,128]{2,1,0:T(8,128)(2,1)} %broadcast_select_fusion.2), calls=%async_computation.1 | async-start | bytes 393216 | tf_op jit(solution)/shard_map/all_to_all | solution.py:95
  56.2 117.3 %all-gather.4.cloned.1.call-start = ((), (), s32[]{:S(2)}) async-start(), calls=%async_computation.10 | async-start | bytes 6488064 | tf_op jit(solution)/shard_map/all_gather | solution.py:124
  69.9 19.3 %copy-start.7 = (bf16[1024,3,128]{0,2,1:T(8,128)(2,1)S(1)}, bf16[1024,3,128]{0,2,1:T(8,128)(2,1)}, u32[]{:S(2)}) copy-start(bf16[1024,3,128]{0,2,1:T(8,128)(2,1)} %copy.116) | copy-start | bytes 2359300
  89.9 86.9 %copy-start.4 = (bf16[384,384]{0,1:T(8,128)(2,1)}, bf16[384,384]{0,1:T(8,128)(2,1)S(1)}, u32[]{:S(2)}) copy-start(bf16[384,384]{0,1:T(8,128)(2,1)S(1)} %convolution_convert_fusion.4) | copy-start | bytes 884740
  182.1 2.8 slice-start
  184.9 70.5 %copy-start.10 = (bf16[128,1024]{1,0:T(8,128)(2,1)S(1)}, bf16[128,1024]{1,0:T(8,128)(2,1)}, u32[]{:S(2)}) copy-start(bf16[128,1024]{1,0:T(8,128)(2,1)} %param.20) | copy-start | bytes 786436
  295.2 16.5 %all-to-all-start.3 = ((bf16[384,8,128]{2,0,1:T(8,128)(2,1)}), bf16[384,8,128]{2,0,1:T(8,128)(2,1)S(1)}, u32[]{:S(2)}, u32[]{:S(2)}) async-start(bf16[384,8,128]{2,0,1:T(8,128)(2,1)} %copy_bitcast_fusion.1), calls=%async_computation.3 | async-start | bytes 1572864 | tf_op jit(solution)/shard_map/all_to_all | solution.py:41
  311.8 14.7 %copy-start.3 = (bf16[384,128]{1,0:T(8,128)(2,1)}, bf16[384,128]{1,0:T(8,128)(2,1)S(1)}, u32[]{:S(2)}) copy-start(bf16[384,128]{1,0:T(8,128)(2,1)S(1)} %add_convert_fusion) | copy-start | bytes 294916
  311.8 14.7 %copy-start.13 = (s32[1152]{0:T(1024)S(1)}, s32[1152]{0:T(1024)}, u32[]{:S(2)}) copy-start(s32[1152]{0:T(1024)} %param.16) | copy-start | bytes 13828
  315.8 19.3 %all-to-all-start.4 = ((bf16[32,24,128]{2,1,0:T(8,128)(2,1)}), bf16[32,24,128]{2,1,0:T(8,128)(2,1)S(1)}, u32[]{:S(2)}, u32[]{:S(2)}) async-start(bf16[32,24,128]{2,1,0:T(8,128)(2,1)} %bitcast.12), calls=%async_computation.4 | async-start | bytes 393216 | tf_op jit(solution)/shard_map/all_to_all | solution.py:176
  325.7 40.2 %all-gather.6.cloned.1.call-start = ((), (), s32[]{:S(2)}) async-start(), calls=%async_computation.11 | async-start | bytes 2654208 | tf_op jit(solution)/shard_map/all_gather | solution.py:180
  335.1 30.8 %copy-start.11 = (bf16[1024,96]{0,1:T(8,128)(2,1)S(1)}, bf16[1024,96]{0,1:T(8,128)(2,1)}, u32[]{:S(2)}) copy-start(bf16[1024,96]{0,1:T(8,128)(2,1)} %param.24) | copy-start | bytes 589828
  339.0 34.0 %copy-start.8 = (bf16[4,7,96,48]{2,3,1,0:T(8,128)(2,1)S(1)}, bf16[4,7,96,48]{2,3,1,0:T(8,128)(2,1)}, u32[]{:S(2)}) copy-start(bf16[4,7,96,48]{2,3,1,0:T(8,128)(2,1)} %param.25) | copy-start | bytes 774148
  368.5 4.6 collective-permute-start
  371.7 4.6 collective-permute-start.1
  389.0 4.6 collective-permute-start.2
  392.1 5.1 %collective-permute-start.3 = (bf16[96,3]{1,0:T(8,128)(2,1)S(1)}, bf16[96,3]{1,0:T(8,128)(2,1)S(1)}, u32[]{:S(2)}, u32[]{:S(2)}) collective-permute-start(bf16[96,3]{1,0:T(8,128)(2,1)S(1)} %get-tuple-element.193), channel_id=1, source_target_pairs={{8,0},{16,8},{24,16},{32,24},{40,32},{48,40},{56,48},{64,56},{72,6... | collective-permute-start | bytes 1736 | tf_op jit(solution)/shard_map/ppermute | solution.py:26
  411.1 6.3 %collective-permute-start.4 = (bf16[96,3]{1,0:T(8,128)(2,1)S(1)}, bf16[96,3]{1,0:T(8,128)(2,1)S(1)}, u32[]{:S(2)}, u32[]{:S(2)}) collective-permute-start(bf16[96,3]{1,0:T(8,128)(2,1)S(1)} %get-tuple-element.189), channel_id=1, source_target_pairs={{0,8},{8,16},{16,24},{24,32},{32,40},{40,48},{48,56},{56,64},{64,7... | collective-permute-start | bytes 1736 | tf_op jit(solution)/shard_map/ppermute | solution.py:23
  415.9 4.9 collective-permute-start.5
  433.4 5.1 %collective-permute-start.6 = (bf16[96,3]{1,0:T(8,128)(2,1)S(1)}, bf16[96,3]{1,0:T(8,128)(2,1)S(1)}, u32[]{:S(2)}, u32[]{:S(2)}) collective-permute-start(bf16[96,3]{1,0:T(8,128)(2,1)S(1)} %get-tuple-element.184), channel_id=1, source_target_pairs={{0,8},{8,16},{16,24},{24,32},{32,40},{40,48},{48,56},{56,64},{64,7... | collective-permute-start | bytes 1736 | tf_op jit(solution)/shard_map/ppermute | solution.py:23
  437.0 4.6 collective-permute-start.7
  443.3 11.2 %copy-start.12 = (bf16[96,1024]{1,0:T(8,128)(2,1)S(1)}, bf16[96,1024]{1,0:T(8,128)(2,1)}, u32[]{:S(2)}) copy-start(bf16[96,1024]{1,0:T(8,128)(2,1)} %param.26) | copy-start | bytes 589828
  457.1 4.4 copy-start.9
  457.1 33.5 %all-to-all-start.9 = ((bf16[8,128,1152]{1,2,0:T(8,128)(2,1)}), bf16[8,128,1152]{1,2,0:T(8,128)(2,1)S(1)}, u32[]{:S(2)}, u32[]{:S(2)}) async-start(bf16[8,128,1152]{1,2,0:T(8,128)(2,1)} %copy_bitcast_fusion), calls=%async_computation.9 | async-start | bytes 4718592 | tf_op jit(solution)/shard_map/all_to_all | solution.py:41
  490.6 1.0 copy-start.5
  490.6 2.1 copy-start.1
Sparse Core Ops, SparseCore 0:
  90.8 82.6 all-gather.3
  339.2 26.7 all-gather.5

commit v2 on v1

--- a/solution.py
+++ b/solution.py
@@ -177,44 +177,65 @@
     back_index = ((kept_before + local_rank) % seq_devices) * capacity + local_rank // seq_devices
     returned = back_in[jnp.clip(back_index, 0, seq_devices * capacity - 1)]
     grid_rows = jnp.where(keep_flags[:, None] == 1, returned, filler[None, :])
-    grid_whole = lax.all_gather(grid_rows, "mp", axis=1, tiled=True)
+    mp_devices = lax.axis_size("mp")
+    mp_index = lax.axis_index("mp")
+    span = frame_count // mp_devices
+    halo = (KW // 2) * BLOCKS
+    own_frames = lax.all_to_all(
+        grid_rows.reshape(mp_devices, span, feature_width), "mp", 0, 2, tiled=True
+    ).reshape(span, mp_devices * feature_width)
+    dec_in_full = lax.all_gather(w_dec_in, "mp", axis=1, tiled=True)
+    conv_full = lax.all_gather(w_conv, "mp", axis=2, tiled=True)
+    dec_out_full = lax.all_gather(w_dec_out, "mp", axis=0, tiled=True)
     activity = lax.dot_general(
-        w_dec_in, grid_whole, (((0,), (1,)), ((), ())), preferred_element_type=jnp.float32
+        dec_in_full, own_frames, (((0,), (1,)), ((), ())), preferred_element_type=jnp.float32
     ).astype(jnp.bfloat16)
-    channels_local = activity.shape[0]
-    groups_local = channels_local // CG
+    both = ("seq", "mp")
+    place = seq_index * mp_devices + mp_index
+    places_total = seq_devices * mp_devices
+    forward = [(i, i + 1) for i in range(places_total - 1)]
+    backward = [(i + 1, i) for i in range(places_total - 1)]
+    low = lax.ppermute(activity[:, span - halo :], both, forward)
+    high = lax.ppermute(activity[:, :halo], both, backward)
+    activity = jnp.concatenate([low, activity, high], axis=1)
+    frame_at = place * span - halo + jnp.arange(span + 2 * halo, dtype=jnp.int32)
+    in_range = (frame_at >= 0) & (frame_at < places_total * span)
+    groups = C // CG
     for block_id in range(BLOCKS):
-        padded = with_halo(activity, (("seq", 1),), KW // 2)
+        width = activity.shape[1] - (KW - 1)
         shifted = jnp.stack(
-            [padded[:, tap_index : tap_index + frame_count] for tap_index in range(KW)], axis=0
-        )
-        shifted = shifted.reshape(KW, groups_local, CG, frame_count)
-        kernel = w_conv[block_id].reshape(KW, groups_local, CG, CG)
+            [activity[:, tap_index : tap_index + width] for tap_index in range(KW)], axis=0
+        ).reshape(KW, groups, CG, width)
+        kernel = conv_full[block_id].reshape(KW, groups, CG, CG)
         conv = jnp.einsum(
             "tgoi,tgif->gof", kernel, shifted, preferred_element_type=jnp.float32
-        ).reshape(channels_local, frame_count)
-        stats = jnp.stack([jnp.sum(conv, axis=0), jnp.sum(conv * conv, axis=0)], axis=0)
-        stats = jnp.sum(gather_all(stats, "mp"), axis=0)
-        channel_sums = stats[0]
-        square_sums = stats[1]
-        centre = channel_sums / C
-        square_mean = square_sums / C
+        ).reshape(C, width)
+        centre = jnp.mean(conv, axis=0)
+        square_mean = jnp.mean(conv * conv, axis=0)
         normal = (conv - centre) * lax.rsqrt(square_mean - centre * centre + NORM_EPSILON)
         result = jax.nn.gelu(normal, approximate=False)
         if block_id > 0:
-            result = result + activity.astype(jnp.float32)
+            result = result + activity[:, KW // 2 : KW // 2 + width].astype(jnp.float32)
+        lower = (block_id + 1) * (KW // 2)
+        result = jnp.where(in_range[lower : lower + width][None, :], result, 0.0)
         activity = result.astype(jnp.bfloat16)
-    predicted = sum_scatter(
-        rounded(
-            lax.dot_general(
-                w_dec_out, activity, (((0,), (0,)), ((), ())), preferred_element_type=jnp.float32
-            )
-        ).astype(jnp.bfloat16),
-        "mp",
-        0,
-    )
-    masked = (1 - keep_flags).astype(jnp.float32)[None, :]
-    pred_error = ((predicted - targets.astype(jnp.float32)) * masked).astype(jnp.bfloat16)
+    part_height = C // mp_devices
+    pieces = jnp.einsum(
+        "jcd,jcf->jdf",
+        dec_out_full.reshape(mp_devices, part_height, -1),
+        activity.reshape(mp_devices, part_height, span),
+        preferred_element_type=jnp.float32,
+    )
+    predicted = jnp.sum(rounded(pieces), axis=0)
+    own_targets = lax.all_to_all(
+        targets.reshape(targets.shape[0], mp_devices, span), "mp", 1, 0, tiled=True
+    ).reshape(-1, span)
+    own_keep = lax.dynamic_slice_in_dim(keep_flags, mp_index * span, span, 0)
+    masked = (1 - own_keep).astype(jnp.float32)[None, :]
+    own_error = ((predicted - own_targets.astype(jnp.float32)) * masked).astype(jnp.bfloat16)
+    pred_error = lax.all_to_all(
+        own_error.reshape(mp_devices, -1, span), "mp", 0, 2, tiled=True
+    ).reshape(-1, frame_count)
     return (student_rows, pred_error)
 
 

time: 508 us -> 499 us (0.982)
  local copies, waits for them, and re-layouts: 52.8 us -> 136 us
  waiting for transfers between devices: 183 us -> 132 us
  blocking collectives: 89.3 us -> 45.7 us
  matrix products: 73.1 us -> 81.7 us
    slice x6 -> x39, local copies, waits for them, and re-layouts: 0.42 us -> 51.2 us  [the longest x1 25.8 us: local(): kernel = conv_full[block_id].reshape(KW, groups, CG, CG)]
    all_to_all x5 -> x1, blocking collectives: 57.9 us -> 12 us  [local(): lax.all_to_all(own_error.reshape(mp_devices, -1, span), 'mp', 0, 2, tiled...]
    unnamed x56 -> x65, local copies, waits for them, and re-layouts: 12.2 us -> 42.1 us
    all_gather x1 -> x3, waiting for transfers between devices: 26.9 us -> 0.06 us  [the longest x1 0.02 us: local(): dec_out_full = lax.all_gather(w_dec_out, 'mp', axis=0, tiled=True)]
    ppermute x8 -> x2, starting transfers between devices: 20 us -> 5.47 us  [the longest x1 3.55 us: local(): low = lax.ppermute(activity[:, span - halo:], both, forward)]
    all_to_all x2, waiting for transfers between devices: 40.3 us -> 26 us  [sum_scatter(): moved = lax.all_to_all(split, axis, dim, dim, tiled=True)]
    ppermute x8 -> x2, waiting for transfers between devices: 13.3 us -> 0.01 us  [the longest x1 0.01 us: local(): low = lax.ppermute(activity[:, span - halo:], both, forward)]
    all_to_all x0 -> x2, starting transfers between devices: none -> 11.3 us  [the longest x1 6.26 us: local(): lax.all_to_all(grid_rows.reshape(mp_devices, span, feature_width), 'mp',...]
  transfers between devices with their start and end apart: 15 -> 13, of which waited for: 11 -> 7; matrix products, arithmetic and copies ran while one was open for 2% -> 43% of each run, Pallas kernels for 0% -> 0%
where the time goes in v2:
time: 499 us; the launch traced here: 493 us
  local copies, waits for them, and re-layouts  136 us (27%)
  waiting for transfers between devices  132 us (26%)
  matrix products  81.7 us (16%)
  starting transfers between devices  56.2 us (11%)
  blocking collectives  45.7 us (9%)
  other arithmetic  25.9 us (5%)
  between operations  14.8 us (3%)
    all_gather x1, waiting for transfers between devices, local(): lax.all_gather(projected[:, feature_width:], 'seq', axis=0, tiled=True)  82.1 us
    unnamed x65, local copies, waits for them, and re-layouts  42.1 us
    dot_general x24, matrix products, advance(): jnp.einsum('qhd,khd->hqk', queries, block_keys, preferred_element_type=jn...  32 us
    dot_general x24, matrix products, advance(): jnp.einsum('hqk,khd->qhd', expo.astype(jnp.bfloat16), block_values, prefe...  31 us
    all_to_all x2, waiting for transfers between devices, sum_scatter(): moved = lax.all_to_all(split, axis, dim, dim, tiled=True)  26 us
    slice x1, local copies, waits for them, and re-layouts, local(): kernel = conv_full[block_id].reshape(KW, groups, CG, CG)  25.8 us
    slice x32, local copies, waits for them, and re-layouts, local(): activity[:, tap_index:tap_index + width]  24 us
    all_gather x1, blocking collectives, local(): gathered = lax.all_gather(packed, 'mp', axis=1, tiled=True)  17.1 us
  transfers between devices with their start and end apart: 13, of which 7 were waited for; matrix products, arithmetic and copies ran while one was open for 43% of the time, Pallas kernels for 0%

profile of v2, /device:TPU:1, one launch (start us, length us, event | category | flops | bytes accessed | tf_op | source)
XLA Modules:
  0.0 492.9 jit_solution(11680369507923139785)
XLA Ops:
  7.2 1.4 reduce_sum.155
  9.9 11.9 %all-to-all-start = ((s32[32,1,1]{2,1,0:T(1,128)}), s32[32,1,1]{2,1,0:T(1,128)S(1)}, u32[]{:S(2)}, u32[]{:S(2)}) async-start(s32[32,1,1]{2,1,0:T(1,128)} %broadcast_in_dim.95), calls=%async_computation | async-start | bytes 32768 | tf_op jit(solution)/shard_map/all_to_all | solution.py:34
  23.6 2.9 scatter_custom_fusion.2
  27.3 3.0 all-to-all-done
  33.1 1.4 subtract_compare_fusion
  34.6 1.4 compare_select_fusion.2
  36.1 6.4 %scatter_custom_fusion = s32[1152]{0:T(1024)S(1)} fusion(s32[1152]{0:T(1024)S(1)} %get-tuple-element.168, s32[1152]{0:T(1024)S(1)} %iota.25, s32[]{:T(128)} %constant.70.clone.1), kind=kCustom, calls=%fused_computation.300 | custom fusion | bytes 4612 | tf_op jit(solution)/shard_map/scatter | solution.py:86
  42.5 4.5 gather_fusion
  47.2 1.9 gather_fusion.1
  49.9 6.3 %all-to-all-start.1 = ((bf16[32,24,128]{2,1,0:T(8,128)(2,1)}), bf16[32,24,128]{2,1,0:T(8,128)(2,1)S(1)}, u32[]{:S(2)}, u32[]{:S(2)}) async-start(bf16[32,24,128]{2,1,0:T(8,128)(2,1)} %broadcast_select_fusion.2), calls=%async_computation.1 | async-start | bytes 393216 | tf_op jit(solution)/shard_map/all_to_all | solution.py:95
  57.8 7.8 %all-to-all-done.1 = bf16[32,24,128]{2,1,0:T(8,128)(2,1)S(1)} async-done(((bf16[32,24,128]{2,1,0:T(8,128)(2,1)}), bf16[32,24,128]{2,1,0:T(8,128)(2,1)S(1)}, u32[]{:S(2)}, u32[]{:S(2)}) %all-to-all-start.1) | async-done | bytes 196640 | tf_op jit(solution)/shard_map/all_to_all | solution.py:95
  65.6 4.2 scatter_custom_fusion.1
  69.9 1.4 gather_fusion.2
  71.3 17.1 %all-gather = bf16[384,1024]{1,0:T(8,128)(2,1)S(1)} all-gather(bf16[384,128]{1,0:T(8,128)(2,1)S(1)} %gather_fusion.2), channel_id=2, replica_groups=mesh['seq'=32,'mp'=8] {'mp'}, dimensions={1}, use_global_device_ids=true | all-gather | bytes 884736 | tf_op jit(solution)/shard_map/all_gather | solution.py:111
  91.3 82.1 %all-gather.6.cloned.1.call-done = bf16[12288,256]{0,1:T(8,128)(2,1)} async-done(((bf16[384,256]{0,1:T(8,128)(2,1)}), bf16[12288,256]{0,1:T(8,128)(2,1)}) %all-gather.6.cloned.1.call-update) | async-done | bytes 6291472 | tf_op jit(solution)/shard_map/all_gather | solution.py:124
  173.4 3.2 fusion.193
  177.9 2.8 copy.199
  182.0 2.8 copy.200
  184.7 70.5 %while.15 = (s32[]{:T(128)}, f32[2,384]{1,0:T(2,128)S(1)}, f32[2,384]{1,0:T(2,128)S(1)}, f32[384,2,64]{0,2,1:T(8,128)S(1)}, bf16[24,512,2,64]{1,3,2,0:T(8,128)(2...) while((s32[]{:T(128)}, f32[2,384]{1,0:T(2,128)S(1)}, ...), condition=%wide.region_12.13_spmd.clone, body=%wide.region_9.12_spmd.clone.sunk | while | flops 103174656 | bytes 5522537 | solution.py:151
  184.7 1.4 bitcast_reduce_fusion.6
  187.7 1.3 bitcast_reduce_fusion.6
  190.6 1.3 bitcast_reduce_fusion.6
  196.5 1.3 bitcast_reduce_fusion.6
  202.4 1.3 bitcast_reduce_fusion.6
  205.3 1.3 bitcast_reduce_fusion.6
  208.3 1.3 bitcast_reduce_fusion.6
  225.9 1.3 bitcast_reduce_fusion.6
  243.5 1.3 bitcast_reduce_fusion.6
  246.4 1.3 bitcast_reduce_fusion.6
  256.7 7.6 %all-to-all-start.2 = ((bf16[384,8,128]{2,0,1:T(8,128)(2,1)}), bf16[384,8,128]{2,0,1:T(8,128)(2,1)S(1)}, u32[]{:S(2)}, u32[]{:S(2)}) async-start(bf16[384,8,128]{2,0,1:T(8,128)(2,1)} %copy_bitcast_fusion.1), calls=%async_computation.2 | async-start | bytes 1572864 | tf_op jit(solution)/shard_map/all_to_all | solution.py:41
  264.3 1.5 copy.218
  265.8 10.6 %all-to-all-done.2 = bf16[384,8,128]{2,0,1:T(8,128)(2,1)S(1)} async-done(((bf16[384,8,128]{2,0,1:T(8,128)(2,1)}), bf16[384,8,128]{2,0,1:T(8,128)(2,1)S(1)}, u32[]{:S(2)}, u32[]{:S(2)}) %all-to-all-start.2) | async-done | bytes 786464 | tf_op jit(solution)/shard_map/all_to_all | solution.py:41
  276.6 16.5 %all_gather.20 = bf16[384,1024]{1,0:T(8,128)(2,1)S(1)} all-gather(bf16[384,128]{1,0:T(8,128)(2,1)S(1)} %add_convert_fusion.1), channel_id=1, replica_groups=mesh['seq'=32,'mp'=8] {'mp'}, dimensions={1}, use_global_device_ids=true | all-gather | bytes 884736 | tf_op jit(solution)/shard_map/all_gather | solution.py:161
  293.7 4.0 convolution_convert_fusion
  298.7 4.6 all-to-all-start.3
  303.3 15.4 %all-to-all-done.3 = bf16[384,8,128]{2,0,1:T(8,128)(2,1)S(1)} async-done(((bf16[384,8,128]{2,0,1:T(8,128)(2,1)}), bf16[384,8,128]{2,0,1:T(8,128)(2,1)S(1)}, u32[]{:S(2)}, u32[]{:S(2)}) %all-to-all-start.3) | async-done | bytes 786464 | tf_op jit(solution)/shard_map/all_to_all | solution.py:41
  318.9 1.4 gather_fusion.3
  320.4 2.5 gather_fusion.4
  322.9 8.8 %all-to-all-start.4 = ((bf16[32,24,128]{2,1,0:T(8,128)(2,1)}), bf16[32,24,128]{2,1,0:T(8,128)(2,1)S(1)}, u32[]{:S(2)}, u32[]{:S(2)}) async-start(bf16[32,24,128]{2,1,0:T(8,128)(2,1)} %bitcast.12), calls=%async_computation.4 | async-start | bytes 393216 | tf_op jit(solution)/shard_map/all_to_all | solution.py:176
  332.7 8.5 %all-to-all-done.4 = bf16[32,24,128]{2,1,0:T(8,128)(2,1)S(1)} async-done(((bf16[32,24,128]{2,1,0:T(8,128)(2,1)}), bf16[32,24,128]{2,1,0:T(8,128)(2,1)S(1)}, u32[]{:S(2)}, u32[]{:S(2)}) %all-to-all-start.4) | async-done | bytes 196640 | tf_op jit(solution)/shard_map/all_to_all | solution.py:176
  341.2 2.9 gather_fusion.5
  345.1 6.3 %all-to-all-start.5 = ((bf16[8,144,128]{2,1,0:T(8,128)(2,1)}), bf16[8,144,128]{2,1,0:T(8,128)(2,1)S(1)}, u32[]{:S(2)}, u32[]{:S(2)}) async-start(bf16[8,144,128]{2,1,0:T(8,128)(2,1)} %broadcast_select_fusion.1), calls=%async_computation.5 | async-start | bytes 589824 | tf_op jit(solution)/shard_map/all_to_all | solution.py:184
  354.8 3.3 all-to-all-done.5
  358.1 5.0 %all-to-all-start.6 = ((bf16[128,8,144]{0,2,1:T(8,128)(2,1)}), bf16[128,8,144]{0,2,1:T(8,128)(2,1)}, u32[]{:S(2)}, u32[]{:S(2)}) async-start(bf16[128,8,144]{0,2,1:T(8,128)(2,1)} %bitcast.75), calls=%async_computation.6 | async-start | bytes 589824 | tf_op jit(solution)/shard_map/all_to_all | solution.py:230
  363.2 2.1 fusion.33
  365.3 3.5 collective-permute-start
  368.9 1.9 collective-permute-start.1
  370.8 25.8 %fusion.194 = (bf16[1,7,768,48]{3,0,1,2:T(2,128)(2,1)S(1)}, bf16[1,7,768,48]{3,0,1,2:T(2,128)(2,1)S(1)}, bf16[1,7,768,48]{3,0,1,2:T(2,128)(2,1)S(1)}, bf16[1,7,768,48]{3,0,1,2:T(2,128)(2,1)S(1)}) fusion(bf16[4,7,768,48]{3,0,1,2:T(4,128)(2,1)} %all-gather.10.cloned.1.call-done), kind=kLoop, calls=%fused_computation.362 | loop fusion | bytes 4128768 | tf_op jit(solution)/shard_map/slice | solution.py:209
  396.6 1.5 copy.271
  398.1 1.4 copy.272
  399.5 1.4 copy.273
  407.8 1.8 constant_dynamic-update-slice_fusion.5
  409.6 1.8 constant_dynamic-update-slice_fusion.4
  414.6 2.9 bitcast_reduce_fusion.4
  426.7 1.8 constant_dynamic-update-slice_fusion.12
  428.6 1.8 constant_dynamic-update-slice_fusion.11
  433.6 2.9 bitcast_reduce_fusion.3
  445.4 1.8 constant_dynamic-update-slice_fusion.19
  447.2 1.8 constant_dynamic-update-slice_fusion.18
  449.0 1.8 constant_dynamic-update-slice_fusion.17
  453.2 2.9 bitcast_reduce_fusion.2
  456.5 1.5 fusion.90
  469.1 2.2 convert_bitcast_fusion
  473.2 12.0 %all_to_all.68 = bf16[8,128,144]{1,2,0:T(8,128)(2,1)S(1)} all-to-all(bf16[8,128,144]{1,2,0:T(8,128)(2,1)S(1)} %copy.255), channel_id=1, replica_groups=mesh['seq'=32,'mp'=8] {'mp'}, dimensions={0} | all-to-all | bytes 589824 | tf_op jit(solution)/shard_map/all_to_all | solution.py:236
  (326 shorter events, 127.3 us)
Async XLA Ops:
  7.2 286.5 %copy-start = (bf16[512,1024]{1,0:T(8,128)(2,1)S(1)}, bf16[512,1024]{1,0:T(8,128)(2,1)}, u32[]{:S(2)}) copy-start(bf16[512,1024]{1,0:T(8,128)(2,1)} %param.22) | copy-start | bytes 3145732
  9.9 20.5 %all-to-all-start = ((s32[32,1,1]{2,1,0:T(1,128)}), s32[32,1,1]{2,1,0:T(1,128)S(1)}, u32[]{:S(2)}, u32[]{:S(2)}) async-start(s32[32,1,1]{2,1,0:T(1,128)} %broadcast_in_dim.95), calls=%async_computation | async-start | bytes 32768 | tf_op jit(solution)/shard_map/all_to_all | solution.py:34
  42.5 4.7 copy-start.2
  47.0 9.3 %copy-start.5 = (bf16[1024,3,128]{2,0,1:T(8,128)(2,1)S(1)}, bf16[1024,3,128]{2,0,1:T(8,128)(2,1)}, u32[]{:S(2)}) copy-start(bf16[1024,3,128]{2,0,1:T(8,128)(2,1)} %param.19) | copy-start | bytes 2359300
  49.9 15.7 %all-to-all-start.1 = ((bf16[32,24,128]{2,1,0:T(8,128)(2,1)}), bf16[32,24,128]{2,1,0:T(8,128)(2,1)S(1)}, u32[]{:S(2)}, u32[]{:S(2)}) async-start(bf16[32,24,128]{2,1,0:T(8,128)(2,1)} %broadcast_select_fusion.2), calls=%async_computation.1 | async-start | bytes 393216 | tf_op jit(solution)/shard_map/all_to_all | solution.py:95
  56.2 117.1 %all-gather.6.cloned.1.call-start = ((), (), s32[]{:S(2)}) async-start(), calls=%async_computation.8 | async-start | bytes 6488064 | tf_op jit(solution)/shard_map/all_gather | solution.py:124
  57.5 31.5 %copy-start.6 = (bf16[1024,3,128]{0,2,1:T(8,128)(2,1)S(1)}, bf16[1024,3,128]{0,2,1:T(8,128)(2,1)}, u32[]{:S(2)}) copy-start(bf16[1024,3,128]{0,2,1:T(8,128)(2,1)} %copy.198) | copy-start | bytes 2359300
  89.7 86.9 %copy-start.4 = (bf16[384,384]{0,1:T(8,128)(2,1)}, bf16[384,384]{0,1:T(8,128)(2,1)S(1)}, u32[]{:S(2)}) copy-start(bf16[384,384]{0,1:T(8,128)(2,1)S(1)} %convolution_convert_fusion.2) | copy-start | bytes 884740
  90.5 272.7 %all-gather.8.cloned.1.call-start = ((), (), s32[]{:S(2)}) async-start(), calls=%async_computation.9 | async-start | bytes 1769472 | tf_op jit(solution)/shard_map/all_gather | solution.py:187
  181.9 2.8 slice-start
  184.7 70.5 %copy-start.9 = (bf16[128,1024]{1,0:T(8,128)(2,1)S(1)}, bf16[128,1024]{1,0:T(8,128)(2,1)}, u32[]{:S(2)}) copy-start(bf16[128,1024]{1,0:T(8,128)(2,1)} %param.20) | copy-start | bytes 786436
  255.2 9.0 %copy-start.7 = (bf16[4,7,96,48]{2,3,1,0:T(8,128)(2,1)S(1)}, bf16[4,7,96,48]{2,3,1,0:T(8,128)(2,1)}, u32[]{:S(2)}) copy-start(bf16[4,7,96,48]{2,3,1,0:T(8,128)(2,1)} %param.25) | copy-start | bytes 774148
  256.7 19.7 %all-to-all-start.2 = ((bf16[384,8,128]{2,0,1:T(8,128)(2,1)}), bf16[384,8,128]{2,0,1:T(8,128)(2,1)S(1)}, u32[]{:S(2)}, u32[]{:S(2)}) async-start(bf16[384,8,128]{2,0,1:T(8,128)(2,1)} %copy_bitcast_fusion.1), calls=%async_computation.2 | async-start | bytes 1572864 | tf_op jit(solution)/shard_map/all_to_all | solution.py:41
  264.3 106.6 %all-gather.10.cloned.1.call-start = ((), (), s32[]{:S(2)}) async-start(), calls=%async_computation.10 | async-start | bytes 6193152 | tf_op jit(solution)/shard_map/all_gather | solution.py:188
  298.7 33.1 %copy-start.10 = (s32[1152]{0:T(1024)S(1)}, s32[1152]{0:T(1024)}, u32[]{:S(2)}) copy-start(s32[1152]{0:T(1024)} %param.16) | copy-start | bytes 13828
  298.7 20.1 %all-to-all-start.3 = ((bf16[384,8,128]{2,0,1:T(8,128)(2,1)}), bf16[384,8,128]{2,0,1:T(8,128)(2,1)S(1)}, u32[]{:S(2)}, u32[]{:S(2)}) async-start(bf16[384,8,128]{2,0,1:T(8,128)(2,1)} %copy_bitcast_fusion), calls=%async_computation.3 | async-start | bytes 1572864 | tf_op jit(solution)/shard_map/all_to_all | solution.py:41
  318.9 25.2 %copy-start.3 = (bf16[384,128]{1,0:T(8,128)(2,1)}, bf16[384,128]{1,0:T(8,128)(2,1)S(1)}, u32[]{:S(2)}) copy-start(bf16[384,128]{1,0:T(8,128)(2,1)S(1)} %add_convert_fusion) | copy-start | bytes 294916
  320.4 32.9 %copy-start.8 = (bf16[128,1152]{1,0:T(8,128)(2,1)S(1)}, bf16[128,1152]{1,0:T(8,128)(2,1)}, u32[]{:S(2)}) copy-start(bf16[128,1152]{1,0:T(8,128)(2,1)} %param.27) | copy-start | bytes 884740
  322.9 18.3 %all-to-all-start.4 = ((bf16[32,24,128]{2,1,0:T(8,128)(2,1)}), bf16[32,24,128]{2,1,0:T(8,128)(2,1)S(1)}, u32[]{:S(2)}, u32[]{:S(2)}) async-start(bf16[32,24,128]{2,1,0:T(8,128)(2,1)} %bitcast.12), calls=%async_computation.4 | async-start | bytes 393216 | tf_op jit(solution)/shard_map/all_to_all | solution.py:176
  345.1 13.0 %all-to-all-start.5 = ((bf16[8,144,128]{2,1,0:T(8,128)(2,1)}), bf16[8,144,128]{2,1,0:T(8,128)(2,1)S(1)}, u32[]{:S(2)}, u32[]{:S(2)}) async-start(bf16[8,144,128]{2,1,0:T(8,128)(2,1)} %broadcast_select_fusion.1), calls=%async_computation.5 | async-start | bytes 589824 | tf_op jit(solution)/shard_map/all_to_all | solution.py:184
  351.3 117.8 %all-gather.12.cloned.1.call-start = ((), (), s32[]{:S(2)}) async-start(), calls=%async_computation.11 | async-start | bytes 1769472 | tf_op jit(solution)/shard_map/all_gather | solution.py:189
  358.1 113.7 %all-to-all-start.6 = ((bf16[128,8,144]{0,2,1:T(8,128)(2,1)}), bf16[128,8,144]{0,2,1:T(8,128)(2,1)}, u32[]{:S(2)}, u32[]{:S(2)}) async-start(bf16[128,8,144]{0,2,1:T(8,128)(2,1)} %bitcast.75), calls=%async_computation.6 | async-start | bytes 589824 | tf_op jit(solution)/shard_map/all_to_all | solution.py:230
  365.3 35.9 %collective-permute-start = (bf16[768,12]{0,1:T(8,128)(2,1)S(1)}, bf16[768,12]{0,1:T(8,128)(2,1)S(1)}, u32[]{:S(2)}, u32[]{:S(2)}) collective-permute-start(bf16[768,12]{0,1:T(8,128)(2,1)S(1)} %get-tuple-element.165), channel_id=1, source_target_pairs={{0,1},{1,2},{2,3},{3,4},{4,5},{5,6},{6,7},{7,8},{8,9},{9,10},{10,1... | collective-permute-start | bytes 55304 | tf_op jit(solution)/shard_map/ppermute | solution.py:198
  368.9 32.3 %collective-permute-start.1 = (bf16[768,12]{0,1:T(8,128)(2,1)S(1)}, bf16[768,12]{0,1:T(8,128)(2,1)S(1)}, u32[]{:S(2)}, u32[]{:S(2)}) collective-permute-start(bf16[768,12]{0,1:T(8,128)(2,1)S(1)} %get-tuple-element.166), channel_id=1, source_target_pairs={{1,0},{2,1},{3,2},{4,3},{5,4},{6,5},{7,6},{8,7},{9,8},{10,9},{11,1... | collective-permute-start | bytes 55304 | tf_op jit(solution)/shard_map/ppermute | solution.py:199
  453.2 3.3 copy-start.13
  466.5 1.1 copy-start.12
  471.3 0.7 copy-start.11
  471.3 14.8 %copy-start.1 = (bf16[512,1024]{1,0:T(8,128)(2,1)S(1)}, bf16[512,1024]{1,0:T(8,128)(2,1)}, u32[]{:S(2)}) copy-start(bf16[512,1024]{1,0:T(8,128)(2,1)} %param.22) | copy-start | bytes 3145732
Sparse Core Ops, SparseCore 0:
  90.6 82.6 all-gather.5
  175.2 31.5 all-gather.7
  266.9 48.2 all-gather.9
  353.7 23.2 all-gather.11

commit v3 on v2

--- a/solution.py
+++ b/solution.py
@@ -185,7 +185,7 @@
         grid_rows.reshape(mp_devices, span, feature_width), "mp", 0, 2, tiled=True
     ).reshape(span, mp_devices * feature_width)
     dec_in_full = lax.all_gather(w_dec_in, "mp", axis=1, tiled=True)
-    conv_full = lax.all_gather(w_conv, "mp", axis=2, tiled=True)
+    conv_full = lax.all_gather(jnp.transpose(w_conv, (0, 2, 3, 1)), "mp", axis=1, tiled=True)
     dec_out_full = lax.all_gather(w_dec_out, "mp", axis=0, tiled=True)
     activity = lax.dot_general(
         dec_in_full, own_frames, (((0,), (1,)), ((), ())), preferred_element_type=jnp.float32
@@ -203,13 +203,15 @@
     groups = C // CG
     for block_id in range(BLOCKS):
         width = activity.shape[1] - (KW - 1)
-        shifted = jnp.stack(
-            [activity[:, tap_index : tap_index + width] for tap_index in range(KW)], axis=0
-        ).reshape(KW, groups, CG, width)
-        kernel = conv_full[block_id].reshape(KW, groups, CG, CG)
-        conv = jnp.einsum(
-            "tgoi,tgif->gof", kernel, shifted, preferred_element_type=jnp.float32
-        ).reshape(C, width)
+        conv = lax.conv_general_dilated(
+            activity[None],
+            conv_full[block_id],
+            (1,),
+            "VALID",
+            dimension_numbers=("NCH", "OIH", "NCH"),
+            feature_group_count=groups,
+            preferred_element_type=jnp.float32,
+        )[0]
         centre = jnp.mean(conv, axis=0)
         square_mean = jnp.mean(conv * conv, axis=0)
         normal = (conv - centre) * lax.rsqrt(square_mean - centre * centre + NORM_EPSILON)

time: 499 us -> 530 us (1.062)
  matrix products: 81.7 us -> 145 us
  local copies, waits for them, and re-layouts: 136 us -> 95.1 us
    conv_general_dilated x0 -> x4, matrix products: none -> 72.3 us  [local(): lax.conv_general_dilated(activity[None], conv_full[block_id], (1,), 'VALI...]
    unnamed x65 -> x39, local copies, waits for them, and re-layouts: 42.1 us -> 12.8 us
    slice x34 -> x7, local copies, waits for them, and re-layouts: 49.9 us -> 21.1 us  [the longest x5 21 us: local(): conv_full[block_id]]
    conv_general_dilated x0 -> x4, local copies, waits for them, and re-layouts: none -> 10.1 us  [local(): lax.conv_general_dilated(activity[None], conv_full[block_id], (1,), 'VALI...]
    dot_general x4 -> x0, matrix products: 9.36 us -> none  [local(): jnp.einsum('tgoi,tgif->gof', kernel, shifted, preferred_element_type=jnp....]
    broadcast_in_dim x0 -> x3, local copies, waits for them, and re-layouts: none -> 7.2 us  [local(): activity[None]]
  transfers between devices with their start and end apart: 13 -> 13, of which waited for: 7 -> 7; matrix products, arithmetic and copies ran while one was open for 43% -> 45% of each run, Pallas kernels for 0% -> 0%
where the time goes in v3:
time: 530 us; the launch traced here: 520 us
  matrix products  145 us (27%)
  waiting for transfers between devices  133 us (25%)
  local copies, waits for them, and re-layouts  95.1 us (18%)
  starting transfers between devices  56.5 us (11%)
  blocking collectives  45.7 us (9%)
  other arithmetic  28.6 us (5%)
  between operations  15 us (3%)
    all_gather x1, waiting for transfers between devices, local(): lax.all_gather(projected[:, feature_width:], 'seq', axis=0, tiled=True)  82.1 us
    conv_general_dilated x4, matrix products, local(): lax.conv_general_dilated(activity[None], conv_full[block_id], (1,), 'VALI...  72.3 us
    dot_general x24, matrix products, advance(): jnp.einsum('qhd,khd->hqk', queries, block_keys, preferred_element_type=jn...  32 us
    dot_general x24, matrix products, advance(): jnp.einsum('hqk,khd->qhd', expo.astype(jnp.bfloat16), block_values, prefe...  31 us
    all_to_all x2, waiting for transfers between devices, sum_scatter(): moved = lax.all_to_all(split, axis, dim, dim, tiled=True)  25.6 us
    slice x5, local copies, waits for them, and re-layouts, local(): conv_full[block_id]  21 us
    all_gather x1, blocking collectives, local(): gathered = lax.all_gather(packed, 'mp', axis=1, tiled=True)  17.1 us
    all_gather x1, blocking collectives, local(): gathered_two = lax.all_gather(first_out, 'mp', axis=1, tiled=True)  16.6 us
  transfers between devices with their start and end apart: 13, of which 7 were waited for; matrix products, arithmetic and copies ran while one was open for 45% of the time, Pallas kernels for 0%

profile of v3, /device:TPU:1, one launch (start us, length us, event | category | flops | bytes accessed | tf_op | source)
XLA Modules:
  0.0 519.6 jit_solution(9177622102279270396)
XLA Ops:
  7.2 1.4 reduce_sum.155
  9.9 11.9 %all-to-all-start = ((s32[32,1,1]{2,1,0:T(1,128)}), s32[32,1,1]{2,1,0:T(1,128)S(1)}, u32[]{:S(2)}, u32[]{:S(2)}) async-start(s32[32,1,1]{2,1,0:T(1,128)} %broadcast_in_dim.152), calls=%async_computation | async-start | bytes 32768 | tf_op jit(solution)/shard_map/all_to_all | solution.py:34
  23.6 2.9 scatter_custom_fusion.2
  27.3 3.0 all-to-all-done
  33.1 1.4 subtract_compare_fusion
  34.6 1.4 compare_select_fusion.2
  36.1 6.4 %scatter_custom_fusion = s32[1152]{0:T(1024)S(1)} fusion(s32[1152]{0:T(1024)S(1)} %get-tuple-element.162, s32[1152]{0:T(1024)S(1)} %iota.25, s32[]{:T(128)} %constant.70.clone.1), kind=kCustom, calls=%fused_computation.269 | custom fusion | bytes 4612 | tf_op jit(solution)/shard_map/scatter | solution.py:86
  42.5 4.5 gather_fusion
  47.2 1.9 gather_fusion.1
  49.9 6.3 %all-to-all-start.1 = ((bf16[32,24,128]{2,1,0:T(8,128)(2,1)}), bf16[32,24,128]{2,1,0:T(8,128)(2,1)S(1)}, u32[]{:S(2)}, u32[]{:S(2)}) async-start(bf16[32,24,128]{2,1,0:T(8,128)(2,1)} %broadcast_select_fusion.2), calls=%async_computation.1 | async-start | bytes 393216 | tf_op jit(solution)/shard_map/all_to_all | solution.py:95
  57.8 7.8 %all-to-all-done.1 = bf16[32,24,128]{2,1,0:T(8,128)(2,1)S(1)} async-done(((bf16[32,24,128]{2,1,0:T(8,128)(2,1)}), bf16[32,24,128]{2,1,0:T(8,128)(2,1)S(1)}, u32[]{:S(2)}, u32[]{:S(2)}) %all-to-all-start.1) | async-done | bytes 196640 | tf_op jit(solution)/shard_map/all_to_all | solution.py:95
  65.6 4.2 scatter_custom_fusion.1
  69.9 1.4 gather_fusion.2
  71.3 17.1 %all-gather = bf16[384,1024]{1,0:T(8,128)(2,1)S(1)} all-gather(bf16[384,128]{1,0:T(8,128)(2,1)S(1)} %gather_fusion.2), channel_id=2, replica_groups=mesh['seq'=32,'mp'=8] {'mp'}, dimensions={1}, use_global_device_ids=true | all-gather | bytes 884736 | tf_op jit(solution)/shard_map/all_gather | solution.py:111
  91.3 82.1 %all-gather.6.cloned.1.call-done = bf16[12288,256]{0,1:T(8,128)(2,1)} async-done(((bf16[384,256]{0,1:T(8,128)(2,1)}), bf16[12288,256]{0,1:T(8,128)(2,1)}) %all-gather.6.cloned.1.call-update) | async-done | bytes 6291472 | tf_op jit(solution)/shard_map/all_gather | solution.py:124
  173.4 3.2 fusion.191
  177.9 2.7 copy.130
  181.9 2.8 copy.131
  184.7 70.5 %while.15 = (s32[]{:T(128)}, f32[2,384]{1,0:T(2,128)S(1)}, f32[2,384]{1,0:T(2,128)S(1)}, f32[384,2,64]{0,2,1:T(8,128)S(1)}, bf16[24,512,2,64]{1,3,2,0:T(8,128)(2...) while((s32[]{:T(128)}, f32[2,384]{1,0:T(2,128)S(1)}, ...), condition=%wide.region_12.13_spmd.clone, body=%wide.region_9.12_spmd.clone.sunk | while | flops 103174656 | bytes 5522537 | solution.py:151
  184.7 1.4 bitcast_reduce_fusion.2
  187.7 1.3 bitcast_reduce_fusion.2
  190.6 1.3 bitcast_reduce_fusion.2
  205.3 1.3 bitcast_reduce_fusion.2
  214.1 1.3 bitcast_reduce_fusion.2
  231.7 1.3 bitcast_reduce_fusion.2
  234.7 1.3 bitcast_reduce_fusion.2
  249.3 1.3 bitcast_reduce_fusion.2
  256.7 7.6 %all-to-all-start.2 = ((bf16[384,8,128]{2,0,1:T(8,128)(2,1)}), bf16[384,8,128]{2,0,1:T(8,128)(2,1)S(1)}, u32[]{:S(2)}, u32[]{:S(2)}) async-start(bf16[384,8,128]{2,0,1:T(8,128)(2,1)} %copy_bitcast_fusion.1), calls=%async_computation.2 | async-start | bytes 1572864 | tf_op jit(solution)/shard_map/all_to_all | solution.py:41
  264.3 1.6 copy.136
  265.9 10.6 %all-to-all-done.2 = bf16[384,8,128]{2,0,1:T(8,128)(2,1)S(1)} async-done(((bf16[384,8,128]{2,0,1:T(8,128)(2,1)}), bf16[384,8,128]{2,0,1:T(8,128)(2,1)S(1)}, u32[]{:S(2)}, u32[]{:S(2)}) %all-to-all-start.2) | async-done | bytes 786464 | tf_op jit(solution)/shard_map/all_to_all | solution.py:41
  276.6 16.6 %all_gather.20 = bf16[384,1024]{1,0:T(8,128)(2,1)S(1)} all-gather(bf16[384,128]{1,0:T(8,128)(2,1)S(1)} %add_convert_fusion.1), channel_id=1, replica_groups=mesh['seq'=32,'mp'=8] {'mp'}, dimensions={1}, use_global_device_ids=true | all-gather | bytes 884736 | tf_op jit(solution)/shard_map/all_gather | solution.py:161
  293.8 4.0 convolution_convert_fusion
  298.9 4.9 all-to-all-start.3
  303.8 15.1 %all-to-all-done.3 = bf16[384,8,128]{2,0,1:T(8,128)(2,1)S(1)} async-done(((bf16[384,8,128]{2,0,1:T(8,128)(2,1)}), bf16[384,8,128]{2,0,1:T(8,128)(2,1)S(1)}, u32[]{:S(2)}, u32[]{:S(2)}) %all-to-all-start.3) | async-done | bytes 786464 | tf_op jit(solution)/shard_map/all_to_all | solution.py:41
  319.0 1.4 gather_fusion.3
  320.5 2.5 gather_fusion.4
  323.0 8.8 %all-to-all-start.4 = ((bf16[32,24,128]{2,1,0:T(8,128)(2,1)}), bf16[32,24,128]{2,1,0:T(8,128)(2,1)S(1)}, u32[]{:S(2)}, u32[]{:S(2)}) async-start(bf16[32,24,128]{2,1,0:T(8,128)(2,1)} %bitcast.12), calls=%async_computation.4 | async-start | bytes 393216 | tf_op jit(solution)/shard_map/all_to_all | solution.py:176
  332.7 8.5 %all-to-all-done.4 = bf16[32,24,128]{2,1,0:T(8,128)(2,1)S(1)} async-done(((bf16[32,24,128]{2,1,0:T(8,128)(2,1)}), bf16[32,24,128]{2,1,0:T(8,128)(2,1)S(1)}, u32[]{:S(2)}, u32[]{:S(2)}) %all-to-all-start.4) | async-done | bytes 196640 | tf_op jit(solution)/shard_map/all_to_all | solution.py:176
  341.3 2.9 gather_fusion.5
  345.1 6.2 %all-to-all-start.5 = ((bf16[8,144,128]{2,1,0:T(8,128)(2,1)}), bf16[8,144,128]{2,1,0:T(8,128)(2,1)S(1)}, u32[]{:S(2)}, u32[]{:S(2)}) async-start(bf16[8,144,128]{2,1,0:T(8,128)(2,1)} %broadcast_select_fusion.1), calls=%async_computation.5 | async-start | bytes 589824 | tf_op jit(solution)/shard_map/all_to_all | solution.py:184
  353.2 4.9 all-to-all-done.5
  358.2 5.0 all-to-all-start.6
  363.3 2.1 fusion.25
  365.4 3.5 collective-permute-start
  368.9 1.9 collective-permute-start.1
  370.9 16.8 %fusion.192 = (bf16[1,768,48,7]{2,0,3,1:T(2,128)(2,1)S(1)}, bf16[1,768,48,7]{2,0,3,1:T(2,128)(2,1)S(1)}, bf16[1,768,48,7]{2,0,3,1:T(2,128)(2,1)S(1)}, bf16[1,768,48,7]{2,0,3,1:T(2,128)(2,1)S(1)}) fusion(bf16[4,768,48,7]{2,0,3,1:T(4,128)(2,1)} %all-gather.10.cloned.1.call-done), kind=kLoop, calls=%fused_computation.336 | loop fusion | bytes 4128768 | tf_op jit(solution)/shard_map/slice | solution.py:208
  389.2 1.3 copy.147
  392.1 2.4 copy.138
  394.5 18.5 %fusion.186 = (f32[162]{0:T(256)S(1)}, f32[162]{0:T(256)S(1)}, f32[1,16,48,162]{2,0,1,3:T(1,128)}) fusion(bf16[1,16,48,168]{2,0,1,3:T(2,128)(2,1)} %copy.138, bf16[16,48,48,7]{2,1,0,3:T(8,128)(2,1)S(1)} %bitcast.168), kind=kOutput, calls=%fused_computation.331 | convolution fusion | flops 83980480 | bytes 1273104 | tf_op jit(solution)/shard_map/conv_general_dilated | solution.py:206
  413.0 2.5 copy.139
  415.6 1.8 fusion.32
  417.4 2.4 copy.141
  420.1 1.7 negate_multiply_fusion.2
  421.9 16.4 %fusion.187 = (f32[156]{0:T(256)S(1)}, f32[156]{0:T(256)S(1)}, f32[1,16,48,156]{2,0,1,3:T(1,128)}) fusion(bf16[1,16,48,162]{2,0,1,3:T(2,128)(2,1)S(1)} %copy-done.8, bf16[16,48,48,7]{2,1,0,3:T(8,128)(2,1)S(1)} %bitcast.167), kind=kOutput, calls=%fused_computation.332 | convolution fusion | flops 80870080 | bytes 1245408 | tf_op jit(solution)/shard_map/conv_general_dilated | solution.py:206
  438.3 2.5 copy.142
  441.9 2.8 fusion.66
  444.9 2.5 copy.148
  447.4 18.5 %fusion.188 = (f32[150]{0:T(256)S(1)}, f32[150]{0:T(256)S(1)}, f32[1,16,48,150]{2,0,1,3:T(1,128)}) fusion(bf16[1,16,48,156]{2,0,1,3:T(2,128)(2,1)} %copy.148, bf16[16,48,48,7]{2,1,0,3:T(8,128)(2,1)S(1)} %bitcast.166), kind=kOutput, calls=%fused_computation.333 | convolution fusion | flops 77759696 | bytes 1217712 | tf_op jit(solution)/shard_map/conv_general_dilated | solution.py:206
  465.9 2.5 copy.149
  470.1 2.3 copy.153
  472.5 18.8 %fusion.189 = (f32[144]{0:T(256)S(1)}, f32[144]{0:T(256)S(1)}, f32[1,16,48,144]{2,0,1,3:T(1,128)}) fusion(bf16[1,16,48,150]{2,0,1,3:T(2,128)(2,1)} %copy.153, bf16[16,48,48,7]{2,1,0,3:T(8,128)(2,1)S(1)} %bitcast.165), kind=kOutput, calls=%fused_computation.334 | convolution fusion | flops 74649312 | bytes 1190016 | tf_op jit(solution)/shard_map/conv_general_dilated | solution.py:206
  491.3 2.5 copy.154
  495.6 2.2 convert_bitcast_fusion
  499.7 12.0 %all_to_all.68 = bf16[8,128,144]{1,2,0:T(8,128)(2,1)S(1)} all-to-all(bf16[8,128,144]{1,2,0:T(8,128)(2,1)S(1)} %copy.159), channel_id=1, replica_groups=mesh['seq'=32,'mp'=8] {'mp'}, dimensions={0} | all-to-all | bytes 589824 | tf_op jit(solution)/shard_map/all_to_all | solution.py:238
  (277 shorter events, 91.6 us)
Async XLA Ops:
  7.2 286.6 %copy-start = (bf16[512,1024]{1,0:T(8,128)(2,1)S(1)}, bf16[512,1024]{1,0:T(8,128)(2,1)}, u32[]{:S(2)}) copy-start(bf16[512,1024]{1,0:T(8,128)(2,1)} %param.22) | copy-start | bytes 3145732
  9.9 20.5 %all-to-all-start = ((s32[32,1,1]{2,1,0:T(1,128)}), s32[32,1,1]{2,1,0:T(1,128)S(1)}, u32[]{:S(2)}, u32[]{:S(2)}) async-start(s32[32,1,1]{2,1,0:T(1,128)} %broadcast_in_dim.152), calls=%async_computation | async-start | bytes 32768 | tf_op jit(solution)/shard_map/all_to_all | solution.py:34
  42.5 4.7 copy-start.2
  47.0 9.3 %copy-start.9 = (bf16[1024,3,128]{2,0,1:T(8,128)(2,1)S(1)}, bf16[1024,3,128]{2,0,1:T(8,128)(2,1)}, u32[]{:S(2)}) copy-start(bf16[1024,3,128]{2,0,1:T(8,128)(2,1)} %param.19) | copy-start | bytes 2359300
  49.9 15.7 %all-to-all-start.1 = ((bf16[32,24,128]{2,1,0:T(8,128)(2,1)}), bf16[32,24,128]{2,1,0:T(8,128)(2,1)S(1)}, u32[]{:S(2)}, u32[]{:S(2)}) async-start(bf16[32,24,128]{2,1,0:T(8,128)(2,1)} %broadcast_select_fusion.2), calls=%async_computation.1 | async-start | bytes 393216 | tf_op jit(solution)/shard_map/all_to_all | solution.py:95
  56.2 117.1 %all-gather.6.cloned.1.call-start = ((), (), s32[]{:S(2)}) async-start(), calls=%async_computation.8 | async-start | bytes 6488064 | tf_op jit(solution)/shard_map/all_gather | solution.py:124
  69.9 19.1 %copy-start.10 = (bf16[1024,3,128]{0,2,1:T(8,128)(2,1)S(1)}, bf16[1024,3,128]{0,2,1:T(8,128)(2,1)}, u32[]{:S(2)}) copy-start(bf16[1024,3,128]{0,2,1:T(8,128)(2,1)} %copy.129) | copy-start | bytes 2359300
  89.7 86.9 %copy-start.4 = (bf16[384,384]{0,1:T(8,128)(2,1)}, bf16[384,384]{0,1:T(8,128)(2,1)S(1)}, u32[]{:S(2)}) copy-start(bf16[384,384]{0,1:T(8,128)(2,1)S(1)} %convolution_convert_fusion.2) | copy-start | bytes 884740
  90.5 272.8 %all-gather.8.cloned.1.call-start = ((), (), s32[]{:S(2)}) async-start(), calls=%async_computation.9 | async-start | bytes 1769472 | tf_op jit(solution)/shard_map/all_gather | solution.py:187
  181.9 2.8 slice-start
  184.7 70.5 %copy-start.13 = (bf16[128,1024]{1,0:T(8,128)(2,1)S(1)}, bf16[128,1024]{1,0:T(8,128)(2,1)}, u32[]{:S(2)}) copy-start(bf16[128,1024]{1,0:T(8,128)(2,1)} %param.20) | copy-start | bytes 786436
  255.6 8.7 %copy-start.11 = (bf16[4,7,96,48]{2,3,1,0:T(8,128)(2,1)S(1)}, bf16[4,7,96,48]{2,3,1,0:T(8,128)(2,1)}, u32[]{:S(2)}) copy-start(bf16[4,7,96,48]{2,3,1,0:T(8,128)(2,1)} %param.25) | copy-start | bytes 774148
  256.7 19.8 %all-to-all-start.2 = ((bf16[384,8,128]{2,0,1:T(8,128)(2,1)}), bf16[384,8,128]{2,0,1:T(8,128)(2,1)S(1)}, u32[]{:S(2)}, u32[]{:S(2)}) async-start(bf16[384,8,128]{2,0,1:T(8,128)(2,1)} %copy_bitcast_fusion.1), calls=%async_computation.2 | async-start | bytes 1572864 | tf_op jit(solution)/shard_map/all_to_all | solution.py:41
  264.3 106.5 %all-gather.10.cloned.1.call-start = ((), (), s32[]{:S(2)}) async-start(), calls=%async_computation.10 | async-start | bytes 6193152 | tf_op jit(solution)/shard_map/all_gather | solution.py:188
  298.9 20.0 %all-to-all-start.3 = ((bf16[384,8,128]{2,0,1:T(8,128)(2,1)}), bf16[384,8,128]{2,0,1:T(8,128)(2,1)S(1)}, u32[]{:S(2)}, u32[]{:S(2)}) async-start(bf16[384,8,128]{2,0,1:T(8,128)(2,1)} %copy_bitcast_fusion), calls=%async_computation.3 | async-start | bytes 1572864 | tf_op jit(solution)/shard_map/all_to_all | solution.py:41
  319.0 25.2 %copy-start.3 = (bf16[384,128]{1,0:T(8,128)(2,1)}, bf16[384,128]{1,0:T(8,128)(2,1)S(1)}, u32[]{:S(2)}) copy-start(bf16[384,128]{1,0:T(8,128)(2,1)S(1)} %add_convert_fusion) | copy-start | bytes 294916
  319.0 12.8 %copy-start.14 = (s32[1152]{0:T(1024)S(1)}, s32[1152]{0:T(1024)}, u32[]{:S(2)}) copy-start(s32[1152]{0:T(1024)} %param.16) | copy-start | bytes 13828
  323.0 18.2 %all-to-all-start.4 = ((bf16[32,24,128]{2,1,0:T(8,128)(2,1)}), bf16[32,24,128]{2,1,0:T(8,128)(2,1)S(1)}, u32[]{:S(2)}, u32[]{:S(2)}) async-start(bf16[32,24,128]{2,1,0:T(8,128)(2,1)} %bitcast.12), calls=%async_computation.4 | async-start | bytes 393216 | tf_op jit(solution)/shard_map/all_to_all | solution.py:176
  341.3 11.0 %copy-start.12 = (bf16[128,1152]{1,0:T(8,128)(2,1)S(1)}, bf16[128,1152]{1,0:T(8,128)(2,1)}, u32[]{:S(2)}) copy-start(bf16[128,1152]{1,0:T(8,128)(2,1)} %param.27) | copy-start | bytes 884740
  345.1 13.0 %all-to-all-start.5 = ((bf16[8,144,128]{2,1,0:T(8,128)(2,1)}), bf16[8,144,128]{2,1,0:T(8,128)(2,1)S(1)}, u32[]{:S(2)}, u32[]{:S(2)}) async-start(bf16[8,144,128]{2,1,0:T(8,128)(2,1)} %broadcast_select_fusion.1), calls=%async_computation.5 | async-start | bytes 589824 | tf_op jit(solution)/shard_map/all_to_all | solution.py:184
  351.4 144.2 %all-gather.12.cloned.1.call-start = ((), (), s32[]{:S(2)}) async-start(), calls=%async_computation.11 | async-start | bytes 1769472 | tf_op jit(solution)/shard_map/all_gather | solution.py:189
  358.2 140.2 %all-to-all-start.6 = ((bf16[128,8,144]{0,2,1:T(8,128)(2,1)}), bf16[128,8,144]{0,2,1:T(8,128)(2,1)}, u32[]{:S(2)}, u32[]{:S(2)}) async-start(bf16[128,8,144]{0,2,1:T(8,128)(2,1)} %bitcast.32), calls=%async_computation.6 | async-start | bytes 589824 | tf_op jit(solution)/shard_map/all_to_all | solution.py:232
  365.4 26.5 %collective-permute-start = (bf16[768,12]{0,1:T(8,128)(2,1)S(1)}, bf16[768,12]{0,1:T(8,128)(2,1)S(1)}, u32[]{:S(2)}, u32[]{:S(2)}) collective-permute-start(bf16[768,12]{0,1:T(8,128)(2,1)S(1)} %get-tuple-element.159), channel_id=1, source_target_pairs={{0,1},{1,2},{2,3},{3,4},{4,5},{5,6},{6,7},{7,8},{8,9},{9,10},{10,1... | collective-permute-start | bytes 55304 | tf_op jit(solution)/shard_map/ppermute | solution.py:198
  368.9 22.9 %collective-permute-start.1 = (bf16[768,12]{0,1:T(8,128)(2,1)S(1)}, bf16[768,12]{0,1:T(8,128)(2,1)S(1)}, u32[]{:S(2)}, u32[]{:S(2)}) collective-permute-start(bf16[768,12]{0,1:T(8,128)(2,1)S(1)} %get-tuple-element.160), channel_id=1, source_target_pairs={{1,0},{2,1},{3,2},{4,3},{5,4},{6,5},{7,6},{8,7},{9,8},{10,9},{11,1... | collective-permute-start | bytes 55304 | tf_op jit(solution)/shard_map/ppermute | solution.py:199
  420.0 1.9 copy-start.7
  420.0 1.9 copy-start.8
  444.7 2.7 copy-start.6
  468.7 3.8 copy-start.5
  498.2 14.4 %copy-start.1 = (bf16[512,1024]{1,0:T(8,128)(2,1)S(1)}, bf16[512,1024]{1,0:T(8,128)(2,1)}, u32[]{:S(2)}) copy-start(bf16[512,1024]{1,0:T(8,128)(2,1)} %param.22) | copy-start | bytes 3145732
Sparse Core Ops, SparseCore 0:
  90.6 82.6 all-gather.5
  175.2 31.5 all-gather.7
  267.0 47.9 all-gather.9
  353.7 23.2 all-gather.11

commit v4 on v2

--- a/solution.py
+++ b/solution.py
@@ -125,7 +125,7 @@
     piece_keys = key_value[:, :feature_width]
     piece_values = key_value[:, feature_width:]
     piece_rows = piece_keys.shape[0]
-    block_rows = math.gcd(piece_rows, 512)
+    block_rows = math.gcd(piece_rows, 1024)
     piece_keys = piece_keys.reshape(piece_rows // block_rows, block_rows, heads_local, HEAD_DIM)
     piece_values = piece_values.reshape(piece_rows // block_rows, block_rows, heads_local, HEAD_DIM)
 
@@ -185,7 +185,7 @@
         grid_rows.reshape(mp_devices, span, feature_width), "mp", 0, 2, tiled=True
     ).reshape(span, mp_devices * feature_width)
     dec_in_full = lax.all_gather(w_dec_in, "mp", axis=1, tiled=True)
-    conv_full = lax.all_gather(w_conv, "mp", axis=2, tiled=True)
+    conv_full = lax.all_gather(jnp.transpose(w_conv, (0, 2, 1, 3)), "mp", axis=1, tiled=True)
     dec_out_full = lax.all_gather(w_dec_out, "mp", axis=0, tiled=True)
     activity = lax.dot_general(
         dec_in_full, own_frames, (((0,), (1,)), ((), ())), preferred_element_type=jnp.float32
@@ -206,9 +206,9 @@
         shifted = jnp.stack(
             [activity[:, tap_index : tap_index + width] for tap_index in range(KW)], axis=0
         ).reshape(KW, groups, CG, width)
-        kernel = conv_full[block_id].reshape(KW, groups, CG, CG)
+        kernel = conv_full[block_id].reshape(groups, CG, KW, CG)
         conv = jnp.einsum(
-            "tgoi,tgif->gof", kernel, shifted, preferred_element_type=jnp.float32
+            "goti,tgif->gof", kernel, shifted, preferred_element_type=jnp.float32
         ).reshape(C, width)
         centre = jnp.mean(conv, axis=0)
         square_mean = jnp.mean(conv * conv, axis=0)

time: 499 us -> 527 us (1.056)
  local copies, waits for them, and re-layouts: 136 us -> 154 us
  matrix products: 81.7 us -> 91.2 us
    reshape x4 -> x6, local copies, waits for them, and re-layouts: 0.95 us -> 13.2 us  [the longest x1 6.11 us: local(): piece_values.reshape(piece_rows // block_rows, block_rows, heads_local, H...]
    dot_general x24 -> x12, matrix products: 32 us -> 38.9 us  [advance(): jnp.einsum('qhd,khd->hqk', queries, block_keys, preferred_element_type=jn...]
    dot_general x24 -> x12, matrix products: 31 us -> 33.5 us  [advance(): jnp.einsum('hqk,khd->qhd', expo.astype(jnp.bfloat16), block_values, prefe...]
    unnamed x65 -> x61, local copies, waits for them, and re-layouts: 42.1 us -> 44.3 us
  transfers between devices with their start and end apart: 13 -> 13, of which waited for: 7 -> 7; matrix products, arithmetic and copies ran while one was open for 43% -> 46% of each run, Pallas kernels for 0% -> 0%
where the time goes in v4:
time: 527 us; the launch traced here: 521 us
  local copies, waits for them, and re-layouts  154 us (29%)
  waiting for transfers between devices  133 us (25%)
  matrix products  91.2 us (17%)
  starting transfers between devices  56.4 us (11%)
  blocking collectives  45.4 us (9%)
  other arithmetic  26.3 us (5%)
  between operations  14.8 us (3%)
    all_gather x1, waiting for transfers between devices, local(): lax.all_gather(projected[:, feature_width:], 'seq', axis=0, tiled=True)  82.1 us
    unnamed x61, local copies, waits for them, and re-layouts  44.3 us
    dot_general x12, matrix products, advance(): jnp.einsum('qhd,khd->hqk', queries, block_keys, preferred_element_type=jn...  38.9 us
    dot_general x12, matrix products, advance(): jnp.einsum('hqk,khd->qhd', expo.astype(jnp.bfloat16), block_values, prefe...  33.5 us
    all_to_all x2, waiting for transfers between devices, sum_scatter(): moved = lax.all_to_all(split, axis, dim, dim, tiled=True)  26 us
    slice x1, local copies, waits for them, and re-layouts, local(): kernel = conv_full[block_id].reshape(groups, CG, KW, CG)  25.5 us
    slice x32, local copies, waits for them, and re-layouts, local(): activity[:, tap_index:tap_index + width]  23.9 us
    all_gather x1, blocking collectives, local(): gathered = lax.all_gather(packed, 'mp', axis=1, tiled=True)  17.1 us
  transfers between devices with their start and end apart: 13, of which 7 were waited for; matrix products, arithmetic and copies ran while one was open for 46% of the time, Pallas kernels for 0%

profile of v4, /device:TPU:1, one launch (start us, length us, event | category | flops | bytes accessed | tf_op | source)
XLA Modules:
  0.0 521.1 jit_solution(13364919659799813224)
XLA Ops:
  9.9 11.9 %all-to-all-start = ((s32[32,1,1]{2,1,0:T(1,128)}), s32[32,1,1]{2,1,0:T(1,128)S(1)}, u32[]{:S(2)}, u32[]{:S(2)}) async-start(s32[32,1,1]{2,1,0:T(1,128)} %broadcast_in_dim.95), calls=%async_computation | async-start | bytes 32768 | tf_op jit(solution)/shard_map/all_to_all | solution.py:34
  23.6 2.9 scatter_custom_fusion.2
  27.3 3.0 all-to-all-done
  36.1 6.4 %scatter_custom_fusion = s32[1152]{0:T(1024)S(1)} fusion(s32[1152]{0:T(1024)S(1)} %get-tuple-element.168, s32[1152]{0:T(1024)S(1)} %iota.25, s32[]{:T(128)} %constant.70.clone.1), kind=kCustom, calls=%fused_computation.301 | custom fusion | bytes 4612 | tf_op jit(solution)/shard_map/scatter | solution.py:86
  42.5 4.5 gather_fusion
  47.2 1.9 gather_fusion.1
  49.9 6.3 %all-to-all-start.1 = ((bf16[32,24,128]{2,1,0:T(8,128)(2,1)}), bf16[32,24,128]{2,1,0:T(8,128)(2,1)S(1)}, u32[]{:S(2)}, u32[]{:S(2)}) async-start(bf16[32,24,128]{2,1,0:T(8,128)(2,1)} %broadcast_select_fusion.2), calls=%async_computation.1 | async-start | bytes 393216 | tf_op jit(solution)/shard_map/all_to_all | solution.py:95
  57.0 8.6 %all-to-all-done.1 = bf16[32,24,128]{2,1,0:T(8,128)(2,1)S(1)} async-done(((bf16[32,24,128]{2,1,0:T(8,128)(2,1)}), bf16[32,24,128]{2,1,0:T(8,128)(2,1)S(1)}, u32[]{:S(2)}, u32[]{:S(2)}) %all-to-all-start.1) | async-done | bytes 196640 | tf_op jit(solution)/shard_map/all_to_all | solution.py:95
  65.6 4.2 scatter_custom_fusion.1
  71.3 17.1 %all-gather = bf16[384,1024]{1,0:T(8,128)(2,1)S(1)} all-gather(bf16[384,128]{1,0:T(8,128)(2,1)S(1)} %gather_fusion.2), channel_id=2, replica_groups=mesh['seq'=32,'mp'=8] {'mp'}, dimensions={1}, use_global_device_ids=true | all-gather | bytes 884736 | tf_op jit(solution)/shard_map/all_gather | solution.py:111
  91.3 82.1 %all-gather.6.cloned.1.call-done = bf16[12288,256]{0,1:T(8,128)(2,1)} async-done(((bf16[384,256]{0,1:T(8,128)(2,1)}), bf16[12288,256]{0,1:T(8,128)(2,1)}) %all-gather.6.cloned.1.call-update) | async-done | bytes 6291472 | tf_op jit(solution)/shard_map/all_gather | solution.py:124
  173.4 6.2 %fusion.200 = (bf16[12288,128]{0,1:T(8,128)(2,1)}, bf16[12288,128]{0,1:T(8,128)(2,1)}) fusion(bf16[12288,256]{0,1:T(8,128)(2,1)} %all-gather.6.cloned.1.call-done), kind=kLoop, calls=%fused_computation.362 | loop fusion | bytes 12582912 | tf_op jit(solution)/shard_map/slice | solution.py:126
  179.6 6.1 %reshape.527 = bf16[12,1024,2,64]{1,0,3,2:T(8,128)(2,1)} reshape(bf16[12288,128]{0,1:T(8,128)(2,1)} %get-tuple-element.132) | data formatting | bytes 6291456 | tf_op jit(solution)/shard_map/reshape | solution.py:129
  185.7 5.6 %copy.199 = bf16[12,1024,2,64]{1,3,2,0:T(8,128)(2,1)} copy(bf16[12,1024,2,64]{1,0,3,2:T(8,128)(2,1)} %reshape.527) | data formatting | bytes 6291456
  191.3 6.1 %reshape.529 = bf16[12,1024,2,64]{1,0,3,2:T(8,128)(2,1)} reshape(bf16[12288,128]{0,1:T(8,128)(2,1)} %get-tuple-element.131) | data formatting | bytes 6291456 | tf_op jit(solution)/shard_map/reshape | solution.py:130
  197.4 5.8 %copy.200 = bf16[12,1024,2,64]{1,3,2,0:T(8,128)(2,1)} copy(bf16[12,1024,2,64]{1,0,3,2:T(8,128)(2,1)} %reshape.529) | data formatting | bytes 6291456
  203.1 80.8 %while.15 = (s32[]{:T(128)}, f32[2,384]{1,0:T(2,128)S(1)}, f32[2,384]{1,0:T(2,128)S(1)}, f32[384,2,64]{0,2,1:T(8,128)S(1)}, bf16[12,1024,2,64]{1,3,2,0:T(8,128)(...) while((s32[]{:T(128)}, f32[2,384]{1,0:T(2,128)S(1)}, ...), condition=%wide.region_12.13_spmd.clone, body=%wide.region_9.12_spmd.clone.sunk | while | flops 207770112 | bytes 23086212 | solution.py:151
  203.1 3.3 bitcast_reduce_fusion.6
  206.4 2.8 fusion.235
  209.9 3.2 bitcast_reduce_fusion.6
  213.1 2.8 fusion.235
  216.6 3.2 bitcast_reduce_fusion.6
  219.9 2.8 fusion.235
  223.3 3.2 bitcast_reduce_fusion.6
  226.6 2.8 fusion.235
  230.1 3.2 bitcast_reduce_fusion.6
  233.3 2.8 fusion.235
  236.8 3.2 bitcast_reduce_fusion.6
  240.1 2.8 fusion.235
  243.5 3.2 bitcast_reduce_fusion.6
  246.8 2.8 fusion.235
  250.3 3.2 bitcast_reduce_fusion.6
  253.5 2.8 fusion.235
  257.0 3.2 bitcast_reduce_fusion.6
  260.2 2.8 fusion.235
  263.7 3.2 bitcast_reduce_fusion.6
  267.0 2.8 fusion.235
  270.4 3.2 bitcast_reduce_fusion.6
  273.7 2.8 fusion.235
  277.2 3.2 bitcast_reduce_fusion.6
  280.4 2.8 fusion.235
  285.4 7.5 %all-to-all-start.2 = ((bf16[384,8,128]{2,0,1:T(8,128)(2,1)}), bf16[384,8,128]{2,0,1:T(8,128)(2,1)S(1)}, u32[]{:S(2)}, u32[]{:S(2)}) async-start(bf16[384,8,128]{2,0,1:T(8,128)(2,1)} %copy_bitcast_fusion.1), calls=%async_computation.2 | async-start | bytes 1572864 | tf_op jit(solution)/shard_map/all_to_all | solution.py:41
  294.5 10.6 %all-to-all-done.2 = bf16[384,8,128]{2,0,1:T(8,128)(2,1)S(1)} async-done(((bf16[384,8,128]{2,0,1:T(8,128)(2,1)}), bf16[384,8,128]{2,0,1:T(8,128)(2,1)S(1)}, u32[]{:S(2)}, u32[]{:S(2)}) %all-to-all-start.2) | async-done | bytes 786464 | tf_op jit(solution)/shard_map/all_to_all | solution.py:41
  305.2 16.3 %all_gather.20 = bf16[384,1024]{1,0:T(8,128)(2,1)S(1)} all-gather(bf16[384,128]{1,0:T(8,128)(2,1)S(1)} %add_convert_fusion.1), channel_id=1, replica_groups=mesh['seq'=32,'mp'=8] {'mp'}, dimensions={1}, use_global_device_ids=true | all-gather | bytes 884736 | tf_op jit(solution)/shard_map/all_gather | solution.py:161
  322.1 4.0 convolution_convert_fusion
  327.2 4.7 all-to-all-start.3
  332.0 15.4 %all-to-all-done.3 = bf16[384,8,128]{2,0,1:T(8,128)(2,1)S(1)} async-done(((bf16[384,8,128]{2,0,1:T(8,128)(2,1)}), bf16[384,8,128]{2,0,1:T(8,128)(2,1)S(1)}, u32[]{:S(2)}, u32[]{:S(2)}) %all-to-all-start.3) | async-done | bytes 786464 | tf_op jit(solution)/shard_map/all_to_all | solution.py:41
  349.1 2.5 gather_fusion.4
  351.6 8.9 %all-to-all-start.4 = ((bf16[32,24,128]{2,1,0:T(8,128)(2,1)}), bf16[32,24,128]{2,1,0:T(8,128)(2,1)S(1)}, u32[]{:S(2)}, u32[]{:S(2)}) async-start(bf16[32,24,128]{2,1,0:T(8,128)(2,1)} %bitcast.12), calls=%async_computation.4 | async-start | bytes 393216 | tf_op jit(solution)/shard_map/all_to_all | solution.py:176
  361.4 8.5 %all-to-all-done.4 = bf16[32,24,128]{2,1,0:T(8,128)(2,1)S(1)} async-done(((bf16[32,24,128]{2,1,0:T(8,128)(2,1)}), bf16[32,24,128]{2,1,0:T(8,128)(2,1)S(1)}, u32[]{:S(2)}, u32[]{:S(2)}) %all-to-all-start.4) | async-done | bytes 196640 | tf_op jit(solution)/shard_map/all_to_all | solution.py:176
  370.0 2.9 gather_fusion.5
  373.8 6.3 %all-to-all-start.5 = ((bf16[8,144,128]{2,1,0:T(8,128)(2,1)}), bf16[8,144,128]{2,1,0:T(8,128)(2,1)S(1)}, u32[]{:S(2)}, u32[]{:S(2)}) async-start(bf16[8,144,128]{2,1,0:T(8,128)(2,1)} %broadcast_select_fusion.1), calls=%async_computation.5 | async-start | bytes 589824 | tf_op jit(solution)/shard_map/all_to_all | solution.py:184
  383.6 3.3 all-to-all-done.5
  386.9 5.0 all-to-all-start.6
  392.0 2.1 fusion.40
  394.1 3.5 collective-permute-start
  397.6 1.9 collective-permute-start.1
  399.6 25.5 %fusion.201 = (bf16[1,768,7,48]{3,0,2,1:T(2,128)(2,1)S(1)}, bf16[1,768,7,48]{3,0,2,1:T(2,128)(2,1)S(1)}, bf16[1,768,7,48]{3,0,2,1:T(2,128)(2,1)S(1)}, bf16[1,768,7,48]{3,0,2,1:T(2,128)(2,1)S(1)}) fusion(bf16[4,768,7,48]{3,0,2,1:T(4,128)(2,1)} %all-gather.10.cloned.1.call-done), kind=kLoop, calls=%fused_computation.363 | loop fusion | bytes 4128768 | tf_op jit(solution)/shard_map/slice | solution.py:209
  436.3 1.8 constant_dynamic-update-slice_fusion.5
  443.1 2.9 bitcast_reduce_fusion.4
  461.9 2.9 bitcast_reduce_fusion.3
  481.5 2.9 bitcast_reduce_fusion.2
  497.4 2.2 convert_bitcast_fusion
  501.5 12.0 %all_to_all.68 = bf16[8,128,144]{1,2,0:T(8,128)(2,1)S(1)} all-to-all(bf16[8,128,144]{1,2,0:T(8,128)(2,1)S(1)} %copy.255), channel_id=1, replica_groups=mesh['seq'=32,'mp'=8] {'mp'}, dimensions={0} | all-to-all | bytes 589824 | tf_op jit(solution)/shard_map/all_to_all | solution.py:236
  (276 shorter events, 101.1 us)
Async XLA Ops:
  7.2 314.9 %copy-start = (bf16[512,1024]{1,0:T(8,128)(2,1)S(1)}, bf16[512,1024]{1,0:T(8,128)(2,1)}, u32[]{:S(2)}) copy-start(bf16[512,1024]{1,0:T(8,128)(2,1)} %param.22) | copy-start | bytes 3145732
  9.9 20.5 %all-to-all-start = ((s32[32,1,1]{2,1,0:T(1,128)}), s32[32,1,1]{2,1,0:T(1,128)S(1)}, u32[]{:S(2)}, u32[]{:S(2)}) async-start(s32[32,1,1]{2,1,0:T(1,128)} %broadcast_in_dim.95), calls=%async_computation | async-start | bytes 32768 | tf_op jit(solution)/shard_map/all_to_all | solution.py:34
  42.5 4.7 copy-start.3
  47.0 9.3 %copy-start.6 = (bf16[1024,3,128]{2,0,1:T(8,128)(2,1)S(1)}, bf16[1024,3,128]{2,0,1:T(8,128)(2,1)}, u32[]{:S(2)}) copy-start(bf16[1024,3,128]{2,0,1:T(8,128)(2,1)} %param.19) | copy-start | bytes 2359300
  49.9 15.7 %all-to-all-start.1 = ((bf16[32,24,128]{2,1,0:T(8,128)(2,1)}), bf16[32,24,128]{2,1,0:T(8,128)(2,1)S(1)}, u32[]{:S(2)}, u32[]{:S(2)}) async-start(bf16[32,24,128]{2,1,0:T(8,128)(2,1)} %broadcast_select_fusion.2), calls=%async_computation.1 | async-start | bytes 393216 | tf_op jit(solution)/shard_map/all_to_all | solution.py:95
  56.2 117.1 %all-gather.6.cloned.1.call-start = ((), (), s32[]{:S(2)}) async-start(), calls=%async_computation.8 | async-start | bytes 6488064 | tf_op jit(solution)/shard_map/all_gather | solution.py:124
  89.7 89.8 %copy-start.5 = (bf16[384,384]{0,1:T(8,128)(2,1)}, bf16[384,384]{0,1:T(8,128)(2,1)S(1)}, u32[]{:S(2)}) copy-start(bf16[384,384]{0,1:T(8,128)(2,1)S(1)} %convolution_convert_fusion.2) | copy-start | bytes 884740
  90.5 301.5 %all-gather.8.cloned.1.call-start = ((), (), s32[]{:S(2)}) async-start(), calls=%async_computation.9 | async-start | bytes 1769472 | tf_op jit(solution)/shard_map/all_gather | solution.py:187
  197.4 5.8 %slice-start = ((bf16[384,384]{0,1:T(8,128)(2,1)}), bf16[384,128]{0,1:T(8,128)(2,1)S(1)}, s32[]{:S(2)}) async-start(bf16[384,384]{0,1:T(8,128)(2,1)} %copy-done.5), calls=%async_computation.12 | async-start | bytes 196608 | tf_op jit(solution)/shard_map/slice | solution.py:116
  203.1 80.8 %copy-start.9 = (bf16[128,1024]{1,0:T(8,128)(2,1)S(1)}, bf16[128,1024]{1,0:T(8,128)(2,1)}, u32[]{:S(2)}) copy-start(bf16[128,1024]{1,0:T(8,128)(2,1)} %param.20) | copy-start | bytes 786436
  206.4 2.9 copy-start.2
  213.1 2.9 copy-start.2
  219.9 2.9 copy-start.2
  226.6 2.9 copy-start.2
  233.3 2.9 copy-start.2
  240.0 2.9 copy-start.2
  246.8 2.9 copy-start.2
  253.5 2.9 copy-start.2
  260.2 2.9 copy-start.2
  267.0 2.9 copy-start.2
  273.7 2.9 copy-start.2
  280.4 2.9 copy-start.2
  283.9 9.0 %copy-start.7 = (bf16[4,7,96,48]{2,3,1,0:T(8,128)(2,1)S(1)}, bf16[4,7,96,48]{2,3,1,0:T(8,128)(2,1)}, u32[]{:S(2)}) copy-start(bf16[4,7,96,48]{2,3,1,0:T(8,128)(2,1)} %param.25) | copy-start | bytes 774148
  285.4 19.7 %all-to-all-start.2 = ((bf16[384,8,128]{2,0,1:T(8,128)(2,1)}), bf16[384,8,128]{2,0,1:T(8,128)(2,1)S(1)}, u32[]{:S(2)}, u32[]{:S(2)}) async-start(bf16[384,8,128]{2,0,1:T(8,128)(2,1)} %copy_bitcast_fusion.1), calls=%async_computation.2 | async-start | bytes 1572864 | tf_op jit(solution)/shard_map/all_to_all | solution.py:41
  292.9 106.7 %all-gather.10.cloned.1.call-start = ((), (), s32[]{:S(2)}) async-start(), calls=%async_computation.10 | async-start | bytes 6193152 | tf_op jit(solution)/shard_map/all_gather | solution.py:188
  327.2 33.3 %copy-start.10 = (s32[1152]{0:T(1024)S(1)}, s32[1152]{0:T(1024)}, u32[]{:S(2)}) copy-start(s32[1152]{0:T(1024)} %param.16) | copy-start | bytes 13828
  327.2 20.2 %all-to-all-start.3 = ((bf16[384,8,128]{2,0,1:T(8,128)(2,1)}), bf16[384,8,128]{2,0,1:T(8,128)(2,1)S(1)}, u32[]{:S(2)}, u32[]{:S(2)}) async-start(bf16[384,8,128]{2,0,1:T(8,128)(2,1)} %copy_bitcast_fusion), calls=%async_computation.3 | async-start | bytes 1572864 | tf_op jit(solution)/shard_map/all_to_all | solution.py:41
  347.6 25.3 %copy-start.4 = (bf16[384,128]{1,0:T(8,128)(2,1)}, bf16[384,128]{1,0:T(8,128)(2,1)S(1)}, u32[]{:S(2)}) copy-start(bf16[384,128]{1,0:T(8,128)(2,1)S(1)} %add_convert_fusion) | copy-start | bytes 294916
  349.0 33.1 %copy-start.8 = (bf16[128,1152]{1,0:T(8,128)(2,1)S(1)}, bf16[128,1152]{1,0:T(8,128)(2,1)}, u32[]{:S(2)}) copy-start(bf16[128,1152]{1,0:T(8,128)(2,1)} %param.27) | copy-start | bytes 884740
  351.6 18.4 %all-to-all-start.4 = ((bf16[32,24,128]{2,1,0:T(8,128)(2,1)}), bf16[32,24,128]{2,1,0:T(8,128)(2,1)S(1)}, u32[]{:S(2)}, u32[]{:S(2)}) async-start(bf16[32,24,128]{2,1,0:T(8,128)(2,1)} %bitcast.12), calls=%async_computation.4 | async-start | bytes 393216 | tf_op jit(solution)/shard_map/all_to_all | solution.py:176
  373.8 13.0 %all-to-all-start.5 = ((bf16[8,144,128]{2,1,0:T(8,128)(2,1)}), bf16[8,144,128]{2,1,0:T(8,128)(2,1)S(1)}, u32[]{:S(2)}, u32[]{:S(2)}) async-start(bf16[8,144,128]{2,1,0:T(8,128)(2,1)} %broadcast_select_fusion.1), calls=%async_computation.5 | async-start | bytes 589824 | tf_op jit(solution)/shard_map/all_to_all | solution.py:184
  380.1 117.3 %all-gather.12.cloned.1.call-start = ((), (), s32[]{:S(2)}) async-start(), calls=%async_computation.11 | async-start | bytes 1769472 | tf_op jit(solution)/shard_map/all_gather | solution.py:189
  386.9 113.3 %all-to-all-start.6 = ((bf16[128,8,144]{0,2,1:T(8,128)(2,1)}), bf16[128,8,144]{0,2,1:T(8,128)(2,1)}, u32[]{:S(2)}, u32[]{:S(2)}) async-start(bf16[128,8,144]{0,2,1:T(8,128)(2,1)} %bitcast.76), calls=%async_computation.6 | async-start | bytes 589824 | tf_op jit(solution)/shard_map/all_to_all | solution.py:230
  394.1 35.6 %collective-permute-start = (bf16[768,12]{0,1:T(8,128)(2,1)S(1)}, bf16[768,12]{0,1:T(8,128)(2,1)S(1)}, u32[]{:S(2)}, u32[]{:S(2)}) collective-permute-start(bf16[768,12]{0,1:T(8,128)(2,1)S(1)} %get-tuple-element.165), channel_id=1, source_target_pairs={{0,1},{1,2},{2,3},{3,4},{4,5},{5,6},{6,7},{7,8},{8,9},{9,10},{10,1... | collective-permute-start | bytes 55304 | tf_op jit(solution)/shard_map/ppermute | solution.py:198
  397.6 32.1 %collective-permute-start.1 = (bf16[768,12]{0,1:T(8,128)(2,1)S(1)}, bf16[768,12]{0,1:T(8,128)(2,1)S(1)}, u32[]{:S(2)}, u32[]{:S(2)}) collective-permute-start(bf16[768,12]{0,1:T(8,128)(2,1)S(1)} %get-tuple-element.166), channel_id=1, source_target_pairs={{1,0},{2,1},{3,2},{4,3},{5,4},{6,5},{7,6},{8,7},{9,8},{10,9},{11,1... | collective-permute-start | bytes 55304 | tf_op jit(solution)/shard_map/ppermute | solution.py:199
  481.5 3.3 copy-start.13
  494.8 1.1 copy-start.12
  499.6 0.6 copy-start.11
  499.6 14.8 %copy-start.1 = (bf16[512,1024]{1,0:T(8,128)(2,1)S(1)}, bf16[512,1024]{1,0:T(8,128)(2,1)}, u32[]{:S(2)}) copy-start(bf16[512,1024]{1,0:T(8,128)(2,1)} %param.22) | copy-start | bytes 3145732
Sparse Core Ops, SparseCore 0:
  90.6 82.6 all-gather.5
  175.2 31.5 all-gather.7
  295.6 48.2 all-gather.9
  382.4 23.2 all-gather.11
